TPU v7x, 256 devices: a whole 4x4x8 slice. The times are simulated.
256 devices in a mesh: row: 32 (over x, z_hi, y), col: 8 (over z_lo, core).
Axes of the slice: x: 4, y: 4, z: 8 (z_hi: 2, z_lo: 4; z = z_hi * 4 + z_lo), core: 2. Of those that a mesh axis runs over, the one named last changes fastest.
Arguments:
- tile_values: bfloat16 [32, 8, 256, 128, 128], P('row', 'col'), may hold values from -0.125 to 0.125
- tile_coords: int32 [32, 8, 2, 256], P('row', 'col'), may hold values from 0 to 63, as said below
- tile_counts: int32 [32, 8], P('row', 'col'), may hold values from 32 to 256, as said below
- features: bfloat16 [8, 32, 256, 256], P('col', 'row'), may hold values from -6 to 6
- weight_matrix: bfloat16 [256, 256], replicated, may hold values from -0.375 to 0.375
- out_grad: bfloat16 [32, 8, 256, 256], P('row', 'col'), may hold values from -6 to 6
Outputs:
- activated: bfloat16 [32, 8, 256, 256], P('row', 'col')
- feature_grad: float32 [8, 32, 256, 256], P('col', 'row')
- weight_grad: float32 [256, 256], replicated
Inputs may be any that keep to these rules, and one draw needn't show every extreme that they name: `tile_coords`: each device's 256 slots name distinct tile positions; the tile row is below 16. `tile_counts`: some device has all 256 slots live.
All inputs are finite; a program needn't handle non-finite values.
Results may differ from a plain program's by a relative error of at most 0.015.
Values may be sent and summed in bfloat16 or wider, within the bound.
No kernel may reach another device: no remote copies, remote signals or barrier semaphores. Data moves between devices by JAX's collectives and lax.ppermute only.
A program may use at most 128 MiB of HBM per device.

v0:
```python
import math

import jax
import jax.numpy as jnp
from jax import lax
from jax.sharding import PartitionSpec as P


def aggregate(values, pick_index, place_index, live_count, source, segments, transposed):
    slot_total = values.shape[0]
    block_size = math.gcd(slot_total, 32)
    tile_side = values.shape[1]
    width = source.shape[2]

    def block_step(block, totals):
        offset = block * block_size
        chosen = lax.dynamic_slice_in_dim(values, offset, block_size, 0)
        picks = lax.dynamic_slice_in_dim(pick_index, offset, block_size, 0)
        places = lax.dynamic_slice_in_dim(place_index, offset, block_size, 0)
        picked = source[picks]
        if transposed:
            products = jnp.einsum(
                "kij,kif->kjf", chosen, picked, preferred_element_type=jnp.float32
            )
        else:
            products = jnp.einsum(
                "kij,kjf->kif", chosen, picked, preferred_element_type=jnp.float32
            )
        is_live = offset + jnp.arange(block_size, dtype=jnp.int32) < live_count
        products = jnp.where(is_live[:, None, None], products, 0.0)
        return totals.at[places].add(products)

    start_totals = jnp.zeros((segments, tile_side, width), jnp.float32)
    upper = (live_count + block_size - 1) // block_size
    return lax.fori_loop(0, upper, block_step, start_totals)


def shards(tile_values, tile_coords, tile_counts, features, weight_matrix, out_grad):
    values = tile_values[0, 0]
    coords = tile_coords[0, 0]
    live_count = tile_counts[0, 0]
    tile_side = values.shape[1]
    sub_rows = features.shape[2]
    width = features.shape[3]
    n_col = lax.axis_size("col")
    row_tiles = n_col * sub_rows // tile_side
    column_block = lax.all_gather(features, "row", axis=1, tiled=True)
    col_source = column_block.reshape(-1, tile_side, width)
    col_tiles = col_source.shape[0]
    partial_value = aggregate(
        values, coords[1], coords[0], live_count, col_source, row_tiles, False
    )
    partial_value = partial_value.reshape(1, n_col, sub_rows, width)
    share = lax.psum_scatter(partial_value, "col", scatter_dimension=1, tiled=True)
    mixed = share.astype(jnp.bfloat16).reshape(sub_rows, width)
    pre = jnp.dot(mixed, weight_matrix, preferred_element_type=jnp.float32)
    sigma = jax.nn.sigmoid(pre)
    activated = (pre * sigma).astype(jnp.bfloat16)
    pre_grad = (
        out_grad.reshape(sub_rows, width).astype(jnp.float32) * sigma * (1.0 + pre * (1.0 - sigma))
    ).astype(jnp.bfloat16)
    weight_terms = jnp.dot(mixed.T, pre_grad, preferred_element_type=jnp.float32)
    own_grad = jnp.dot(pre_grad, weight_matrix.T, preferred_element_type=jnp.float32).astype(
        jnp.bfloat16
    )
    mixed_grad = lax.all_gather(own_grad.reshape(1, 1, sub_rows, width), "col", axis=1, tiled=True)
    row_source = mixed_grad.reshape(row_tiles, tile_side, width)
    back_partial = aggregate(values, coords[0], coords[1], live_count, row_source, col_tiles, True)
    back_partial = back_partial.reshape(1, -1, sub_rows, width)
    feature_grad = lax.psum_scatter(back_partial, "row", scatter_dimension=1, tiled=True)
    weight_grad = lax.psum(weight_terms, ("row", "col"))
    return (activated.reshape(1, 1, sub_rows, width), feature_grad, weight_grad)


def solution(mesh):
    return jax.shard_map(
        shards,
        mesh=mesh,
        in_specs=(
            P("row", "col", None, None, None),
            P("row", "col", None, None),
            P("row", "col"),
            P("col", "row", None, None),
            P(),
            P("row", "col", None, None),
        ),
        out_specs=(P("row", "col", None, None), P("col", "row", None, None), P()),
        check_vma=False,
    )
```

profile of v0, /device:TPU:72, one launch (start us, length us, event | category | flops | bytes accessed | tf_op | source)
XLA Modules:
  0.0 849.4 jit_solution(18019783541457873077)
XLA Ops:
  7.2 0.0 copy-start
  7.2 0.0 all-gather.4.cloned.1.call-start
  7.2 0.7 all-gather.4.cloned.1.call-update
  7.9 0.0 reduce-scatter.3.cloned.1.call-start
  8.6 0.8 fusion.13
  9.4 112.8 %all-gather.4.cloned.1.call-done = bf16[1,32,256,256]{3,2,0,1:T(8,128)(2,1)} async-done(((bf16[1,1,256,256]{3,2,0,1:T(8,128)(2,1)}), bf16[1,32,256,256]{3,2,0,1:T(8,128)(2,1)}) %all-gather.4.cloned.1.call-update) | async-done | bytes 4194320 | tf_op jit(solution)/shard_map/all_gather | solution.py:47
  122.2 0.2 broadcast_in_dim.40
  122.4 0.0 copy-start.4
  122.4 16.1 %while.20 = (s32[]{:T(128)}, f32[16,128,256]{2,1,0:T(8,128)S(1)}, s32[]{:T(128)}, s32[256]{0:T(256)S(1)}, s32[]{:T(128)}, /*index=5*/bf16[256,128,128]{2,1,0:T(8...) while((s32[]{:T(128)}, f32[16,128,256]{2,1,0:T(8,128)S(1)}, ...), condition=%wide.region_2.3_spmd, body=%wide.region_0.2_spmd.sunk | while | flops 270533888 | bytes 24122484 | solution.py:35
  122.4 0.7 add_compare_fusion.4
  123.1 0.1 compare_select_fusion.6
  123.2 4.2 gather_fusion
  127.4 4.6 convolution_select_fusion.4
  132.0 6.5 scatter_fusion
  138.5 0.0 copy-start.1
  138.5 1.3 copy-done.1
  139.9 0.0 reduce-scatter.3.cloned.1.call-update
  139.9 0.0 all-gather.6.cloned.1.call-start
  139.9 143.9 %reduce-scatter.3.cloned.1.call-done = f32[1,1,256,256]{3,2,1,0:T(8,128)} async-done(((f32[1,8,256,256]{3,2,1,0:T(8,128)}), f32[1,1,256,256]{3,2,1,0:T(8,128)}) %reduce-scatter.3.cloned.1.call-update) | async-done | bytes 262160 | tf_op jit(solution)/shard_map/reduce_scatter | solution.py:54
  283.8 0.0 copy-done
  283.8 0.0 copy-done.4
  283.8 1.9 fusion.5
  285.7 0.9 convolution_convert_fusion
  286.6 0.0 all-gather.6.cloned.1.call-update
  286.6 0.0 all-reduce.2.cloned.1.call-start
  286.6 0.0 copy-start.3
  286.7 12.0 %copy.11 = bf16[1,1,256,128,128]{3,4,2,1,0:T(8,128)(2,1)} copy(bf16[1,1,256,128,128]{4,3,2,1,0:T(8,128)(2,1)} %bitcast.38) | data formatting | bytes 16777216 | tf_op args[0]
  298.7 0.0 copy-done.3
  298.7 0.9 fusion.6
  299.6 0.0 all-reduce.2.cloned.1.call-update
  299.6 0.0 reduce-scatter.5.cloned.1.call-start
  299.7 23.9 %all-gather.6.cloned.1.call-done = bf16[2048,256]{1,0:T(8,128)(2,1)} async-done(((bf16[256,256]{1,0:T(8,128)(2,1)}), bf16[2048,256]{1,0:T(8,128)(2,1)}) %all-gather.6.cloned.1.call-update) | async-done | bytes 1048592 | tf_op jit(solution)/shard_map/all_gather | solution.py:66
  323.6 0.0 copy-start.2
  323.6 4.3 broadcast_in_dim.41
  327.9 0.0 copy-done.2
  327.9 15.3 %while.21 = (s32[]{:T(128)}, f32[64,128,256]{2,1,0:T(8,128)}, s32[]{:T(128)}, s32[256]{0:T(256)S(1)}, s32[]{:T(128)}, /*index=5*/bf16[256,128,128]{1,2,0:T(8,128...) while((s32[]{:T(128)}, f32[64,128,256]{2,1,0:T(8,128)}, ...), condition=%wide.region_6.7_spmd, body=%wide.region_4.6_spmd.sunk | while | flops 270533888 | bytes 24122484 | solution.py:35
  327.9 0.7 add_compare_fusion.5
  328.6 0.1 compare_select_fusion.7
  328.6 0.7 gather_fusion.1
  329.3 3.9 convolution_select_fusion.5
  333.2 10.0 %scatter_fusion.1 = f32[64,128,256]{2,1,0:T(8,128)} fusion(f32[64,128,256]{2,1,0:T(8,128)} %get-tuple-element.304, s32[32]{0:T(128)S(1)} %get-tuple-element.253, f32[32,128,256]{2,1,0:T(8,128)} %convolution_select_fusion.5), kind=kCustom, calls=%fused_computation.3.clone.1 | custom fusion | flops 1048576 | bytes 12583040 | tf_op jit(solution)/shard_map/while/body/scatter-add | solution.py:31
  343.2 0.0 reduce-scatter.5.cloned.1.call-update
  343.3 241.5 %all-reduce.2.cloned.1.call-done = f32[256,256]{1,0:T(8,128)} async-done(((f32[256,256]{1,0:T(8,128)}), f32[256,256]{1,0:T(8,128)}) %all-reduce.2.cloned.1.call-update) | async-done | bytes 262160 | tf_op jit(solution)/shard_map/psum | solution.py:71
  584.8 256.4 %reduce-scatter.5.cloned.1.call-done = f32[1,1,256,256]{3,2,1,0:T(8,128)} async-done(((f32[1,32,256,256]{3,2,1,0:T(8,128)}), f32[1,1,256,256]{3,2,1,0:T(8,128)}) %reduce-scatter.5.cloned.1.call-update) | async-done | bytes 262160 | tf_op jit(solution)/shard_map/reduce_scatter | solution.py:70
  841.2 1.7 copy.31
  (2 shorter events, 0.0 us)
Async XLA Ops:
  7.2 276.6 %copy-start = (bf16[256,256]{1,0:T(8,128)(2,1)S(1)}, bf16[256,256]{1,0:T(8,128)(2,1)}, u32[]{:S(2)}) copy-start(bf16[256,256]{1,0:T(8,128)(2,1)} %param.14) | copy-start | bytes 393220
  7.2 115.0 %all-gather.4.cloned.1.call-start = ((), (), s32[]{:S(2)}) async-start(), calls=%async_computation.2 | async-start | bytes 4325376 | tf_op jit(solution)/shard_map/all_gather | solution.py:47
  7.9 275.9 %reduce-scatter.3.cloned.1.call-start = ((), (), s32[]{:S(2)}) async-start(), calls=%async_computation.3 | async-start | bytes 2359296 | tf_op jit(solution)/shard_map/reduce_scatter | solution.py:54
  122.4 161.4 %copy-start.4 = (bf16[1,1,256,256]{3,2,1,0:T(8,128)(2,1)S(1)}, bf16[1,1,256,256]{3,2,1,0:T(8,128)(2,1)}, u32[]{:S(2)}) copy-start(bf16[1,1,256,256]{3,2,1,0:T(8,128)(2,1)} %param.15) | copy-start | bytes 393220
  138.5 1.3 copy-start.1
  139.9 183.8 %all-gather.6.cloned.1.call-start = ((), (), s32[]{:S(2)}) async-start(), calls=%async_computation.6 | async-start | bytes 1179648 | tf_op jit(solution)/shard_map/all_gather | solution.py:66
  286.6 298.2 %all-reduce.2.cloned.1.call-start = ((), (), s32[]{:S(2)}) async-start(), calls=%async_computation.5 | async-start | bytes 524288 | tf_op jit(solution)/shard_map/psum | solution.py:71
  286.6 12.0 %copy-start.3 = (f32[1,1,256,256]{3,2,1,0:T(8,128)S(1)}, f32[1,1,256,256]{3,2,1,0:T(8,128)}, u32[]{:S(2)}) copy-start(f32[1,1,256,256]{3,2,1,0:T(8,128)} %reduce-scatter.3.cloned.1.call-done) | copy-start | bytes 786436
  299.6 541.6 %reduce-scatter.5.cloned.1.call-start = ((), (), s32[]{:S(2)}) async-start(), calls=%async_computation.4 | async-start | bytes 8650752 | tf_op jit(solution)/shard_map/reduce_scatter | solution.py:70
  323.6 4.3 copy-start.2
Sparse Core Ops, SparseCore 0:
  11.5 110.6 all-gather.3
  140.0 143.7 reduce-scatter.2
  286.7 36.8 all-gather.5
  329.5 255.2 all-reduce.1
  587.8 253.4 reduce-scatter.4
where the time goes:
time: 866 us; the launch traced here: 849 us
  waiting for transfers between devices  779 us (90%)
  local copies, waits for them, and re-layouts  25.2 us (3%)
  other arithmetic  18 us (2%)
  between operations  14.5 us (2%)
  matrix products  12.2 us (1%)
    reduce_scatter x1, waiting for transfers between devices, shards(): lax.psum_scatter(back_partial, 'row', scatter_dimension=1, tiled=True)  256 us
    psum x1, waiting for transfers between devices, shards(): weight_grad = lax.psum(weight_terms, ('row', 'col'))  242 us
    reduce_scatter x1, waiting for transfers between devices, shards(): lax.psum_scatter(partial_value, 'col', scatter_dimension=1, tiled=True)  144 us
    all_gather x1, waiting for transfers between devices, shards(): column_block = lax.all_gather(features, 'row', axis=1, tiled=True)  113 us
    all_gather x1, waiting for transfers between devices, shards(): lax.all_gather(own_grad.reshape(1, 1, sub_rows, width), 'col', axis=1, ti...  23.9 us
  transfers between devices with their start and end apart: 5, of which 5 were waited for; matrix products, arithmetic and copies ran while one was open for 4% of the time, Pallas kernels for 0%

commit v1 on v0

--- a/solution.py
+++ b/solution.py
@@ -35,6 +35,21 @@
     return lax.fori_loop(0, upper, block_step, start_totals)
 
 
+def scatter_sum(partial, axis_name):
+    received = lax.all_to_all(partial, axis_name, 0, 0, tiled=True)
+    return jnp.sum(received.astype(jnp.float32), axis=0)
+
+
+def all_sum(terms):
+    axes = ("row", "col")
+    count = lax.axis_size("row") * lax.axis_size("col")
+    rows, width = terms.shape
+    pieces = terms.reshape(count, rows // count, width)
+    mine = jnp.sum(lax.all_to_all(pieces, axes, 0, 0, tiled=True), axis=0, keepdims=True)
+    spread = jnp.broadcast_to(mine, (count, rows // count, width))
+    return lax.all_to_all(spread, axes, 0, 0, tiled=True).reshape(rows, width)
+
+
 def shards(tile_values, tile_coords, tile_counts, features, weight_matrix, out_grad):
     values = tile_values[0, 0]
     coords = tile_coords[0, 0]
@@ -43,6 +58,7 @@
     sub_rows = features.shape[2]
     width = features.shape[3]
     n_col = lax.axis_size("col")
+    n_row = lax.axis_size("row")
     row_tiles = n_col * sub_rows // tile_side
     column_block = lax.all_gather(features, "row", axis=1, tiled=True)
     col_source = column_block.reshape(-1, tile_side, width)
@@ -50,8 +66,8 @@
     partial_value = aggregate(
         values, coords[1], coords[0], live_count, col_source, row_tiles, False
     )
-    partial_value = partial_value.reshape(1, n_col, sub_rows, width)
-    share = lax.psum_scatter(partial_value, "col", scatter_dimension=1, tiled=True)
+    partial_value = partial_value.reshape(n_col, sub_rows, width)
+    share = scatter_sum(partial_value, "col")
     mixed = share.astype(jnp.bfloat16).reshape(sub_rows, width)
     pre = jnp.dot(mixed, weight_matrix, preferred_element_type=jnp.float32)
     sigma = jax.nn.sigmoid(pre)
@@ -64,11 +80,11 @@
         jnp.bfloat16
     )
     mixed_grad = lax.all_gather(own_grad.reshape(1, 1, sub_rows, width), "col", axis=1, tiled=True)
+    weight_grad = all_sum(weight_terms)
     row_source = mixed_grad.reshape(row_tiles, tile_side, width)
     back_partial = aggregate(values, coords[0], coords[1], live_count, row_source, col_tiles, True)
-    back_partial = back_partial.reshape(1, -1, sub_rows, width)
-    feature_grad = lax.psum_scatter(back_partial, "row", scatter_dimension=1, tiled=True)
-    weight_grad = lax.psum(weight_terms, ("row", "col"))
+    back_partial = back_partial.reshape(n_row, sub_rows, width).astype(jnp.bfloat16)
+    feature_grad = scatter_sum(back_partial, "row").reshape(1, 1, sub_rows, width)
     return (activated.reshape(1, 1, sub_rows, width), feature_grad, weight_grad)
 
 

time: 866 us -> 608 us (0.70); the launches traced: 849 us -> 601 us
  waiting for transfers between devices: 779 us -> 215 us
  starting transfers between devices: 0.2 us -> 191 us
  blocking collectives: 0 us -> 83.2 us
  other arithmetic: 18 us -> 48.5 us
    reduce_scatter x2 -> x0, waiting for transfers between devices: 400 us -> none  [the longest x1 256 us: shards(): lax.psum_scatter(back_partial, 'row', scatter_dimension=1, tiled=True)]
    psum x1 -> x0, waiting for transfers between devices: 242 us -> none  [shards(): weight_grad = lax.psum(weight_terms, ('row', 'col'))]
    all_to_all x0 -> x3, starting transfers between devices: none -> 191 us  [the longest x1 106 us: scatter_sum(): received = lax.all_to_all(partial, axis_name, 0, 0, tiled=True)]
    all_to_all x0 -> x3, waiting for transfers between devices: none -> 101 us  [the longest x1 97.7 us: scatter_sum(): received = lax.all_to_all(partial, axis_name, 0, 0, tiled=True)]
    all_to_all x0 -> x1, blocking collectives: none -> 83.2 us  [scatter_sum(): received = lax.all_to_all(partial, axis_name, 0, 0, tiled=True)]
    all_gather x1, waiting for transfers between devices: 23.9 us -> 0.02 us  [shards(): lax.all_gather(own_grad.reshape(1, 1, sub_rows, width), 'col', axis=1, ti...]
    scatter-add x2 -> x4, other arithmetic: 16.5 us -> 33 us  [block_step(): return totals.at[places].add(products)]
  transfers between devices with their start and end apart: 5 -> 5, of which waited for: 5 -> 3; matrix products, arithmetic and copies ran while one was open for 4% -> 10% of each run, Pallas kernels for 0% -> 0%
where the time goes in v1:
time: 608 us; the launch traced here: 601 us
  waiting for transfers between devices  215 us (35%)
  starting transfers between devices  191 us (31%)
  blocking collectives  83.2 us (14%)
  other arithmetic  48.5 us (8%)
  local copies, waits for them, and re-layouts  29.6 us (5%)
  matrix products  18.9 us (3%)
  between operations  14.8 us (2%)
    all_gather x1, waiting for transfers between devices, shards(): column_block = lax.all_gather(features, 'row', axis=1, tiled=True)  113 us
    all_to_all x1, starting transfers between devices, scatter_sum(): received = lax.all_to_all(partial, axis_name, 0, 0, tiled=True)  106 us
    all_to_all x1, waiting for transfers between devices, scatter_sum(): received = lax.all_to_all(partial, axis_name, 0, 0, tiled=True)  97.7 us
    all_to_all x1, blocking collectives, scatter_sum(): received = lax.all_to_all(partial, axis_name, 0, 0, tiled=True)  83.2 us
    all_to_all x1, starting transfers between devices, all_sum(): lax.all_to_all(pieces, axes, 0, 0, tiled=True)  74.6 us
    scatter-add x4, other arithmetic, block_step(): return totals.at[places].add(products)  33 us
    unnamed x8, local copies, waits for them, and re-layouts  12.8 us
  transfers between devices with their start and end apart: 5, of which 3 were waited for; matrix products, arithmetic and copies ran while one was open for 10% of the time, Pallas kernels for 0%

profile of v1, /device:TPU:72, one launch (start us, length us, event | category | flops | bytes accessed | tf_op | source)
XLA Modules:
  0.0 601.0 jit_solution(6878164607066905335)
XLA Ops:
  7.2 0.0 copy-start
  7.2 0.0 all-gather.4.cloned.1.call-start
  7.2 0.7 all-gather.4.cloned.1.call-update
  7.9 0.0 all-gather.6.cloned.1.call-start
  8.6 0.8 fusion.10
  9.4 112.8 %all-gather.4.cloned.1.call-done = bf16[1,32,256,256]{3,2,0,1:T(8,128)(2,1)} async-done(((bf16[1,1,256,256]{3,2,0,1:T(8,128)(2,1)}), bf16[1,32,256,256]{3,2,0,1:T(8,128)(2,1)}) %all-gather.4.cloned.1.call-update) | async-done | bytes 4194320 | tf_op jit(solution)/shard_map/all_gather | solution.py:63
  122.2 0.2 broadcast_in_dim.46
  122.4 32.2 %while.20 = (s32[]{:T(128)}, f32[16,128,256]{2,1,0:T(8,128)S(1)}, s32[]{:T(128)}, s32[256]{0:T(256)S(1)}, s32[]{:T(128)}, /*index=5*/bf16[256,128,128]{2,1,0:T(8...) while((s32[]{:T(128)}, f32[16,128,256]{2,1,0:T(8,128)S(1)}, ...), condition=%wide.region_2.3_spmd, body=%wide.region_0.2_spmd.sunk | while | flops 270533888 | bytes 24122484 | solution.py:35
  122.4 0.7 add_compare_fusion.4
  123.1 0.1 compare_select_fusion.6
  123.2 4.2 gather_fusion
  127.4 4.6 convolution_select_fusion.4
  132.0 6.5 %scatter_fusion = f32[16,128,256]{2,1,0:T(8,128)S(1)} fusion(f32[16,128,256]{2,1,0:T(8,128)S(1)} %get-tuple-element.268, s32[32]{0:T(128)S(1)} %get-tuple-element.243, f32[32,128,256]{2,1,0:T(8,128)} %convolution_select_fusion.4), kind=kCustom, calls=%fused_computation.2.clone.1 | custom fusion | flops 1048576 | bytes 12583040 | tf_op jit(solution)/shard_map/while/body/scatter-add | solution.py:31
  138.5 0.7 add_compare_fusion.4
  139.2 0.1 compare_select_fusion.6
  139.3 4.2 gather_fusion
  143.5 4.6 convolution_select_fusion.4
  148.1 6.5 %scatter_fusion = f32[16,128,256]{2,1,0:T(8,128)S(1)} fusion(f32[16,128,256]{2,1,0:T(8,128)S(1)} %get-tuple-element.268, s32[32]{0:T(128)S(1)} %get-tuple-element.243, f32[32,128,256]{2,1,0:T(8,128)} %convolution_select_fusion.4), kind=kCustom, calls=%fused_computation.2.clone.1 | custom fusion | flops 1048576 | bytes 12583040 | tf_op jit(solution)/shard_map/while/body/scatter-add | solution.py:31
  154.6 0.0 copy-start.2
  154.6 83.2 %all_to_all.20 = f32[8,256,256]{2,1,0:T(8,128)} all-to-all(f32[8,256,256]{2,1,0:T(8,128)S(1)} %bitcast.34), channel_id=1, replica_groups=mesh['row'=32,'col'=8] {'col'}, dimensions={0} | all-to-all | bytes 4194304 | tf_op jit(solution)/shard_map/all_to_all | solution.py:39
  237.8 1.7 reduce_sum.27
  239.5 0.0 copy-done
  239.5 0.0 copy-done.2
  239.5 0.9 fusion.5
  240.5 0.9 convolution_convert_fusion
  241.3 0.0 all-gather.6.cloned.1.call-update
  241.4 0.2 convolution_bitcast_fusion
  241.6 1.0 copy.14
  242.6 74.6 %all-to-all-start.2 = ((f32[256,1,256]{2,1,0:T(1,128)}), f32[256,1,256]{2,1,0:T(1,128)S(1)}, u32[]{:S(2)}, u32[]{:S(2)}) async-start(f32[256,1,256]{2,1,0:T(1,128)} %copy.14), calls=%async_computation.2 | async-start | bytes 524288 | tf_op jit(solution)/shard_map/all_to_all | solution.py:48
  317.2 12.0 %copy.11 = bf16[1,1,256,128,128]{3,4,2,1,0:T(8,128)(2,1)} copy(bf16[1,1,256,128,128]{4,3,2,1,0:T(8,128)(2,1)} %bitcast.38) | data formatting | bytes 16777216 | tf_op args[0]
  329.2 3.4 all-to-all-done.2
  332.6 0.3 reduce_sum.29
  332.9 0.8 broadcast_in_dim.48
  333.8 10.3 %all-to-all-start.3 = ((f32[256,1,256]{2,1,0:T(1,128)}), f32[256,1,256]{2,1,0:T(1,128)S(1)}, u32[]{:S(2)}, u32[]{:S(2)}) async-start(f32[256,1,256]{2,1,0:T(1,128)} %broadcast_in_dim.48), calls=%async_computation.3 | async-start | bytes 524288 | tf_op jit(solution)/shard_map/all_to_all | solution.py:50
  344.0 0.0 all-gather.6.cloned.1.call-done
  344.1 0.0 copy-start.1
  344.1 4.3 broadcast_in_dim.47
  348.3 0.0 copy-done.1
  348.3 31.7 %while.21 = (s32[]{:T(128)}, f32[64,128,256]{2,1,0:T(8,128)}, s32[]{:T(128)}, s32[256]{0:T(256)S(1)}, s32[]{:T(128)}, /*index=5*/bf16[256,128,128]{1,2,0:T(8,128...) while((s32[]{:T(128)}, f32[64,128,256]{2,1,0:T(8,128)}, ...), condition=%wide.region_6.7_spmd, body=%wide.region_4.6_spmd.sunk | while | flops 270533888 | bytes 24122964 | solution.py:35
  348.3 1.2 add_compare_fusion.5
  349.5 0.1 compare_select_fusion.7
  349.6 0.7 gather_fusion.1
  350.3 3.9 convolution_select_fusion.5
  354.1 10.0 %scatter_fusion.1 = f32[64,128,256]{2,1,0:T(8,128)} fusion(f32[64,128,256]{2,1,0:T(8,128)} %get-tuple-element.304, s32[32]{0:T(128)S(1)} %get-tuple-element.253, f32[32,128,256]{2,1,0:T(8,128)} %convolution_select_fusion.5), kind=kCustom, calls=%fused_computation.3.clone.1 | custom fusion | flops 1048576 | bytes 12583040 | tf_op jit(solution)/shard_map/while/body/scatter-add | solution.py:31
  364.1 1.2 add_compare_fusion.5
  365.3 0.1 compare_select_fusion.7
  365.4 0.7 gather_fusion.1
  366.1 3.9 convolution_select_fusion.5
  369.9 10.1 %scatter_fusion.1 = f32[64,128,256]{2,1,0:T(8,128)} fusion(f32[64,128,256]{2,1,0:T(8,128)} %get-tuple-element.304, s32[32]{0:T(128)S(1)} %get-tuple-element.253, f32[32,128,256]{2,1,0:T(8,128)} %convolution_select_fusion.5), kind=kCustom, calls=%fused_computation.3.clone.1 | custom fusion | flops 1048576 | bytes 12583040 | tf_op jit(solution)/shard_map/while/body/scatter-add | solution.py:31
  380.0 5.9 convert_element_type.33
  385.9 0.0 all-to-all-done.3
  385.9 106.2 %all-to-all-start.1 = ((bf16[32,256,256]{2,1,0:T(8,128)(2,1)}), bf16[32,256,256]{2,1,0:T(8,128)(2,1)}, u32[]{:S(2)}, u32[]{:S(2)}) async-start(bf16[32,256,256]{2,1,0:T(8,128)(2,1)} %bitcast.40), calls=%async_computation.1 | async-start | bytes 8388608 | tf_op jit(solution)/shard_map/all_to_all | solution.py:39
  492.2 0.7 copy.18
  492.9 97.7 %all-to-all-done.1 = bf16[32,256,256]{2,1,0:T(8,128)(2,1)} async-done(((bf16[32,256,256]{2,1,0:T(8,128)(2,1)}), bf16[32,256,256]{2,1,0:T(8,128)(2,1)}, u32[]{:S(2)}, u32[]{:S(2)}) %all-to-all-start.1) | async-done | bytes 4194336 | tf_op jit(solution)/shard_map/all_to_all | solution.py:39
  590.6 3.5 convert_reduce_fusion
  (4 shorter events, 0.0 us)
Async XLA Ops:
  7.2 232.3 %copy-start = (bf16[256,256]{1,0:T(8,128)(2,1)S(1)}, bf16[256,256]{1,0:T(8,128)(2,1)}, u32[]{:S(2)}) copy-start(bf16[256,256]{1,0:T(8,128)(2,1)} %param.14) | copy-start | bytes 393220
  7.2 115.0 %all-gather.4.cloned.1.call-start = ((), (), s32[]{:S(2)}) async-start(), calls=%async_computation.4 | async-start | bytes 4325376 | tf_op jit(solution)/shard_map/all_gather | solution.py:63
  7.9 336.1 %all-gather.6.cloned.1.call-start = ((), (), s32[]{:S(2)}) async-start(), calls=%async_computation.5 | async-start | bytes 1179648 | tf_op jit(solution)/shard_map/all_gather | solution.py:82
  154.6 85.0 %copy-start.2 = (bf16[1,1,256,256]{3,2,1,0:T(8,128)(2,1)S(1)}, bf16[1,1,256,256]{3,2,1,0:T(8,128)(2,1)}, u32[]{:S(2)}) copy-start(bf16[1,1,256,256]{3,2,1,0:T(8,128)(2,1)} %param.15) | copy-start | bytes 393220
  242.6 90.1 %all-to-all-start.2 = ((f32[256,1,256]{2,1,0:T(1,128)}), f32[256,1,256]{2,1,0:T(1,128)S(1)}, u32[]{:S(2)}, u32[]{:S(2)}) async-start(f32[256,1,256]{2,1,0:T(1,128)} %copy.14), calls=%async_computation.2 | async-start | bytes 524288 | tf_op jit(solution)/shard_map/all_to_all | solution.py:48
  333.8 52.2 %all-to-all-start.3 = ((f32[256,1,256]{2,1,0:T(1,128)}), f32[256,1,256]{2,1,0:T(1,128)S(1)}, u32[]{:S(2)}, u32[]{:S(2)}) async-start(f32[256,1,256]{2,1,0:T(1,128)} %broadcast_in_dim.48), calls=%async_computation.3 | async-start | bytes 524288 | tf_op jit(solution)/shard_map/all_to_all | solution.py:50
  344.1 4.3 copy-start.1
  385.9 204.7 %all-to-all-start.1 = ((bf16[32,256,256]{2,1,0:T(8,128)(2,1)}), bf16[32,256,256]{2,1,0:T(8,128)(2,1)}, u32[]{:S(2)}, u32[]{:S(2)}) async-start(bf16[32,256,256]{2,1,0:T(8,128)(2,1)} %bitcast.40), calls=%async_computation.1 | async-start | bytes 8388608 | tf_op jit(solution)/shard_map/all_to_all | solution.py:39
Sparse Core Ops, SparseCore 0:
  11.5 110.6 all-gather.3
  241.5 95.3 all-gather.5

commit v2 on v1

--- a/solution.py
+++ b/solution.py
@@ -1,38 +1,74 @@
-import math
-
 import jax
 import jax.numpy as jnp
 from jax import lax
+from jax.experimental import pallas as pl
+from jax.experimental.pallas import tpu as pltpu
 from jax.sharding import PartitionSpec as P
 
+GROUP = 32
 
-def aggregate(values, pick_index, place_index, live_count, source, segments, transposed):
-    slot_total = values.shape[0]
-    block_size = math.gcd(slot_total, 32)
-    tile_side = values.shape[1]
+
+def tile_aggregate(values, pick_index, place_index, live_count, source, segments, transposed, out_dtype):
+    slot_total, tile_side, _ = values.shape
     width = source.shape[2]
+    steps = slot_total // GROUP
 
-    def block_step(block, totals):
-        offset = block * block_size
-        chosen = lax.dynamic_slice_in_dim(values, offset, block_size, 0)
-        picks = lax.dynamic_slice_in_dim(pick_index, offset, block_size, 0)
-        places = lax.dynamic_slice_in_dim(place_index, offset, block_size, 0)
-        picked = source[picks]
-        if transposed:
-            products = jnp.einsum(
-                "kij,kif->kjf", chosen, picked, preferred_element_type=jnp.float32
-            )
-        else:
-            products = jnp.einsum(
-                "kij,kjf->kif", chosen, picked, preferred_element_type=jnp.float32
-            )
-        is_live = offset + jnp.arange(block_size, dtype=jnp.int32) < live_count
-        products = jnp.where(is_live[:, None, None], products, 0.0)
-        return totals.at[places].add(products)
+    def kernel(picks_ref, places_ref, count_ref, vals_ref, src_ref, out_ref, acc_ref):
+        step = pl.program_id(0)
 
-    start_totals = jnp.zeros((segments, tile_side, width), jnp.float32)
-    upper = (live_count + block_size - 1) // block_size
-    return lax.fori_loop(0, upper, block_step, start_totals)
+        @pl.when(step == 0)
+        def _():
+            acc_ref[...] = jnp.zeros_like(acc_ref)
+
+        def slot(j, carry):
+            k = step * GROUP + j
+
+            @pl.when(k < count_ref[0])
+            def _():
+                src_tile = src_ref[picks_ref[k]]
+                tile = vals_ref[j]
+                if transposed:
+                    term = lax.dot_general(tile, src_tile, (((0,), (0,)), ((), ())),
+                                           preferred_element_type=jnp.float32)
+                else:
+                    term = jnp.dot(tile, src_tile, preferred_element_type=jnp.float32)
+                place = places_ref[k]
+                acc_ref[place] += term
+
+            return carry
+
+        lax.fori_loop(0, GROUP, slot, 0)
+
+        @pl.when(step == steps - 1)
+        def _():
+            out_ref[...] = acc_ref[...].astype(out_ref.dtype)
+
+    def vals_map(i, picks, places, count):
+        return (jnp.minimum(i, (count[0] - 1) // GROUP), 0, 0)
+
+    grid_spec = pltpu.PrefetchScalarGridSpec(
+        num_scalar_prefetch=3,
+        grid=(steps,),
+        in_specs=[
+            pl.BlockSpec((GROUP, tile_side, tile_side), vals_map),
+            pl.BlockSpec(source.shape, lambda i, *_: (0, 0, 0)),
+        ],
+        out_specs=pl.BlockSpec((segments, tile_side, width), lambda i, *_: (0, 0, 0)),
+        scratch_shapes=[pltpu.VMEM((segments, tile_side, width), jnp.float32)],
+    )
+    flops = 2 * slot_total * tile_side * tile_side * width
+    return pl.pallas_call(
+        kernel,
+        grid_spec=grid_spec,
+        out_shape=jax.ShapeDtypeStruct((segments, tile_side, width), out_dtype),
+        compiler_params=pltpu.CompilerParams(
+            dimension_semantics=("arbitrary",), vmem_limit_bytes=48 * 1024 * 1024
+        ),
+        cost_estimate=pl.CostEstimate(
+            flops=flops, transcendentals=0,
+            bytes_accessed=values.size * 2 + source.size * 2 + segments * tile_side * width * jnp.dtype(out_dtype).itemsize,
+        ),
+    )(pick_index, place_index, live_count.reshape(1), values, source)
 
 
 def scatter_sum(partial, axis_name):
@@ -63,8 +99,8 @@
     column_block = lax.all_gather(features, "row", axis=1, tiled=True)
     col_source = column_block.reshape(-1, tile_side, width)
     col_tiles = col_source.shape[0]
-    partial_value = aggregate(
-        values, coords[1], coords[0], live_count, col_source, row_tiles, False
+    partial_value = tile_aggregate(
+        values, coords[1], coords[0], live_count, col_source, row_tiles, False, jnp.float32
     )
     partial_value = partial_value.reshape(n_col, sub_rows, width)
     share = scatter_sum(partial_value, "col")
@@ -82,8 +118,10 @@
     mixed_grad = lax.all_gather(own_grad.reshape(1, 1, sub_rows, width), "col", axis=1, tiled=True)
     weight_grad = all_sum(weight_terms)
     row_source = mixed_grad.reshape(row_tiles, tile_side, width)
-    back_partial = aggregate(values, coords[0], coords[1], live_count, row_source, col_tiles, True)
-    back_partial = back_partial.reshape(n_row, sub_rows, width).astype(jnp.bfloat16)
+    back_partial = tile_aggregate(
+        values, coords[0], coords[1], live_count, row_source, col_tiles, True, jnp.bfloat16
+    )
+    back_partial = back_partial.reshape(n_row, sub_rows, width)
     feature_grad = scatter_sum(back_partial, "row").reshape(1, 1, sub_rows, width)
     return (activated.reshape(1, 1, sub_rows, width), feature_grad, weight_grad)
 

time: 608 us -> 435 us (0.72)
  starting transfers between devices: 191 us -> 61.7 us
  other arithmetic: 48.5 us -> 3.91 us
  blocking collectives: 83.2 us -> 108 us
  Pallas kernels: 0 us -> 24.3 us
  local copies, waits for them, and re-layouts: 29.6 us -> 5.81 us
  matrix products: 18.9 us -> 2.04 us
    all_to_all x1 -> x0, starting transfers between devices: 74.6 us -> none  [all_sum(): lax.all_to_all(pieces, axes, 0, 0, tiled=True)]
    all_to_all x1, starting transfers between devices: 106 us -> 53.2 us  [scatter_sum(): received = lax.all_to_all(partial, axis_name, 0, 0, tiled=True)]
    scatter-add x4 -> x0, other arithmetic: 33 us -> none  [block_step(): return totals.at[places].add(products)]
    all_to_all x0 -> x1, blocking collectives: none -> 30.2 us  [all_sum(): lax.all_to_all(pieces, axes, 0, 0, tiled=True)]
    pallas_call x0 -> x2, Pallas kernels: none -> 24.3 us  [tile_aggregate(): pl.pallas_call(kernel, grid_spec=grid_spec, out_shape=jax.ShapeDtypeStruc...]
    dot_general x4 -> x0, matrix products: 16.9 us -> none  [the longest x2 9.17 us: block_step(): jnp.einsum('kij,kjf->kif', chosen, picked, preferred_element_type=jnp.flo...]
    gather x4 -> x0, local copies, waits for them, and re-layouts: 9.81 us -> none  [block_step(): picked = source[picks]]
    unnamed x8 -> x9, local copies, waits for them, and re-layouts: 12.8 us -> 3.93 us
  transfers between devices with their start and end apart: 5 -> 4, of which waited for: 3 -> 2; matrix products, arithmetic and copies ran while one was open for 10% -> 1% of each run, Pallas kernels for 0% -> 3%
where the time goes in v2:
time: 435 us; the launch traced here: 432 us
  waiting for transfers between devices  211 us (49%)
  blocking collectives  108 us (25%)
  starting transfers between devices  61.7 us (14%)
  Pallas kernels  24.3 us (6%)
  between operations  14.8 us (3%)
  local copies, waits for them, and re-layouts  5.81 us (1%)
    all_gather x1, waiting for transfers between devices, shards(): column_block = lax.all_gather(features, 'row', axis=1, tiled=True)  113 us
    all_to_all x1, waiting for transfers between devices, scatter_sum(): received = lax.all_to_all(partial, axis_name, 0, 0, tiled=True)  97.5 us
    all_to_all x1, blocking collectives, scatter_sum(): received = lax.all_to_all(partial, axis_name, 0, 0, tiled=True)  77.9 us
    all_to_all x1, starting transfers between devices, scatter_sum(): received = lax.all_to_all(partial, axis_name, 0, 0, tiled=True)  53.2 us
    all_to_all x1, blocking collectives, all_sum(): lax.all_to_all(pieces, axes, 0, 0, tiled=True)  30.2 us
    pallas_call x2, Pallas kernels, tile_aggregate(): pl.pallas_call(kernel, grid_spec=grid_spec, out_shape=jax.ShapeDtypeStruc...  24.3 us
  transfers between devices with their start and end apart: 4, of which 2 were waited for; matrix products, arithmetic and copies ran while one was open for 1% of the time, Pallas kernels for 3%

profile of v2, /device:TPU:72, one launch (start us, length us, event | category | flops | bytes accessed | tf_op | source)
XLA Modules:
  0.0 431.7 jit_solution(5824178768911457029)
XLA Ops:
  7.2 0.0 copy-start
  7.2 0.0 all-gather.4.cloned.1.call-start
  7.2 0.7 all-gather.4.cloned.1.call-update
  7.9 0.0 all-gather.6.cloned.1.call-start
  8.6 0.8 fusion.6
  9.4 112.8 %all-gather.4.cloned.1.call-done = bf16[1,32,256,256]{3,2,0,1:T(8,128)(2,1)} async-done(((bf16[1,1,256,256]{3,2,0,1:T(8,128)(2,1)}), bf16[1,32,256,256]{3,2,0,1:T(8,128)(2,1)}) %all-gather.4.cloned.1.call-update) | async-done | bytes 4194320 | tf_op jit(solution)/shard_map/all_gather | solution.py:99
  122.2 11.8 %shard_map.85 = f32[16,128,256]{2,1,0:T(8,128)S(1)} custom-call(s32[256]{0:T(256)S(1)} %bitcast.33, s32[256]{0:T(256)S(1)} %bitcast.31, s32[1]{0:T(128)} %bitcast.26.count_ref, bf16[256,128,128]{2,1,0:T(8,128)(2,1)} %bitcast.35, bf16[64,128,256]{2,1,0:T(8,128)(2,1)} %bitcast.37), custom_call_target="tpu_custom_call" | custom-call | flops 2147483648 | bytes 14680064 | tf_op jit(solution)/shard_map/pallas_call | solution.py:60
  134.0 0.0 copy-start.3
  134.0 77.9 %all_to_all.20 = f32[8,256,256]{2,1,0:T(8,128)S(1)} all-to-all(f32[8,256,256]{2,1,0:T(8,128)S(1)} %bitcast.29), channel_id=1, replica_groups=mesh['row'=32,'col'=8] {'col'}, dimensions={0} | all-to-all | bytes 4194304 | tf_op jit(solution)/shard_map/all_to_all | solution.py:75
  211.9 0.1 reduce_sum.27
  212.0 0.0 copy-done
  212.0 0.0 copy-done.3
  212.0 0.9 fusion.1
  213.0 0.9 convolution_convert_fusion
  213.8 0.0 all-gather.6.cloned.1.call-update
  213.9 0.2 convolution_bitcast_fusion
  214.1 0.3 copy.10
  214.4 30.2 %all_to_all.21 = f32[256,1,256]{2,1,0:T(1,128)S(1)} all-to-all(f32[256,1,256]{2,1,0:T(1,128)S(1)} %copy.10), channel_id=1, replica_groups=mesh['row'=32,'col'=8] {'row','col'}, dimensions={0} | all-to-all | bytes 524288 | tf_op jit(solution)/shard_map/all_to_all | solution.py:84
  244.6 0.3 reduce_sum.29
  244.9 0.8 broadcast_in_dim.2
  245.7 8.4 %all-to-all-start.3 = ((f32[256,1,256]{2,1,0:T(1,128)}), f32[256,1,256]{2,1,0:T(1,128)S(1)}, u32[]{:S(2)}, u32[]{:S(2)}) async-start(f32[256,1,256]{2,1,0:T(1,128)} %broadcast_in_dim.2), calls=%async_computation.3 | async-start | bytes 524288 | tf_op jit(solution)/shard_map/all_to_all | solution.py:86
  254.1 0.0 all-gather.6.cloned.1.call-done
  254.2 0.0 copy-start.2
  254.2 1.2 copy-done.2
  255.4 12.5 %shard_map.86 = bf16[64,128,256]{2,1,0:T(8,128)(2,1)S(1)} custom-call(s32[256]{0:T(256)S(1)} %bitcast.32, s32[256]{0:T(256)S(1)} %bitcast.34, s32[1]{0:T(128)} %bitcast.27.count_ref, bf16[256,128,128]{2,1,0:T(8,128)(2,1)} %bitcast.36, bf16[16,128,256]{2,1,0:T(8,128)(2,1)S(1)} %bitcast.30), custom_call_target="tpu_custom_call" | custom-call | flops 2147483648 | bytes 13631488 | tf_op jit(solution)/shard_map/pallas_call | solution.py:60
  267.9 0.0 copy-start.1
  267.9 2.0 copy-done.1
  269.9 0.0 all-to-all-done.3
  269.9 53.2 %all-to-all-start.1 = ((bf16[32,256,256]{2,1,0:T(8,128)(2,1)}), bf16[32,256,256]{2,1,0:T(8,128)(2,1)}, u32[]{:S(2)}, u32[]{:S(2)}) async-start(bf16[32,256,256]{2,1,0:T(8,128)(2,1)} %bitcast.28), calls=%async_computation.1 | async-start | bytes 8388608 | tf_op jit(solution)/shard_map/all_to_all | solution.py:75
  323.1 0.7 copy.13
  323.8 97.5 %all-to-all-done.1 = bf16[32,256,256]{2,1,0:T(8,128)(2,1)} async-done(((bf16[32,256,256]{2,1,0:T(8,128)(2,1)}), bf16[32,256,256]{2,1,0:T(8,128)(2,1)}, u32[]{:S(2)}, u32[]{:S(2)}) %all-to-all-start.1) | async-done | bytes 4194336 | tf_op jit(solution)/shard_map/all_to_all | solution.py:75
  421.3 3.5 convert_reduce_fusion
Async XLA Ops:
  7.2 204.8 %copy-start = (bf16[256,256]{1,0:T(8,128)(2,1)S(1)}, bf16[256,256]{1,0:T(8,128)(2,1)}, u32[]{:S(2)}) copy-start(bf16[256,256]{1,0:T(8,128)(2,1)} %param.10) | copy-start | bytes 393220
  7.2 115.0 %all-gather.4.cloned.1.call-start = ((), (), s32[]{:S(2)}) async-start(), calls=%async_computation.4 | async-start | bytes 4325376 | tf_op jit(solution)/shard_map/all_gather | solution.py:99
  7.9 246.2 %all-gather.6.cloned.1.call-start = ((), (), s32[]{:S(2)}) async-start(), calls=%async_computation.5 | async-start | bytes 1179648 | tf_op jit(solution)/shard_map/all_gather | solution.py:118
  134.0 78.1 %copy-start.3 = (bf16[1,1,256,256]{3,2,1,0:T(8,128)(2,1)S(1)}, bf16[1,1,256,256]{3,2,1,0:T(8,128)(2,1)}, u32[]{:S(2)}) copy-start(bf16[1,1,256,256]{3,2,1,0:T(8,128)(2,1)} %param.11) | copy-start | bytes 393220
  245.7 24.2 %all-to-all-start.3 = ((f32[256,1,256]{2,1,0:T(1,128)}), f32[256,1,256]{2,1,0:T(1,128)S(1)}, u32[]{:S(2)}, u32[]{:S(2)}) async-start(f32[256,1,256]{2,1,0:T(1,128)} %broadcast_in_dim.2), calls=%async_computation.3 | async-start | bytes 524288 | tf_op jit(solution)/shard_map/all_to_all | solution.py:86
  254.2 1.2 copy-start.2
  267.9 2.0 copy-start.1
  269.9 151.4 %all-to-all-start.1 = ((bf16[32,256,256]{2,1,0:T(8,128)(2,1)}), bf16[32,256,256]{2,1,0:T(8,128)(2,1)}, u32[]{:S(2)}, u32[]{:S(2)}) async-start(bf16[32,256,256]{2,1,0:T(8,128)(2,1)} %bitcast.28), calls=%async_computation.1 | async-start | bytes 8388608 | tf_op jit(solution)/shard_map/all_to_all | solution.py:75
Sparse Core Ops, SparseCore 0:
  11.5 110.6 all-gather.3
  214.0 35.7 all-gather.5

commit v3 on v2

--- a/solution.py
+++ b/solution.py
@@ -76,6 +76,62 @@
     return jnp.sum(received.astype(jnp.float32), axis=0)
 
 
+def ring_step_pairs(size, stride, digits, shift):
+    pairs = []
+    for index in range(size):
+        digit = (index // stride) % digits
+        pairs.append((index, index + (((digit + shift) % digits) - digit) * stride))
+    return pairs
+
+
+def ring_reduce(partial, axis_name, stride, link_dtype):
+    digits = partial.shape[0]
+    size = lax.axis_size(axis_name)
+    digit = (lax.axis_index(axis_name) // stride) % digits
+    half = partial.shape[1] // 2
+    lead = partial.shape[1]
+
+    def block(offset):
+        return lax.dynamic_index_in_dim(partial, (digit + offset) % digits, 0, keepdims=False)
+
+    rightward = ring_step_pairs(size, stride, digits, 1)
+    leftward = ring_step_pairs(size, stride, digits, -1)
+    far = block(2)
+    to_right = jnp.concatenate([block(1), far[:half]]).astype(link_dtype)
+    to_left = jnp.concatenate([block(digits - 1), far[half:]]).astype(link_dtype)
+    from_left = lax.ppermute(to_right, axis_name, rightward)
+    from_right = lax.ppermute(to_left, axis_name, leftward)
+    relay_left = lax.ppermute(from_left[lead:], axis_name, rightward)
+    relay_right = lax.ppermute(from_right[lead:], axis_name, leftward)
+    total = block(0).astype(jnp.float32) + from_left[:lead].astype(jnp.float32)
+    total = total + from_right[:lead].astype(jnp.float32)
+    return total + jnp.concatenate([relay_left, relay_right]).astype(jnp.float32)
+
+
+def pair_reduce(partial, axis_name, stride, link_dtype):
+    size = lax.axis_size(axis_name)
+    digit = (lax.axis_index(axis_name) // stride) % 2
+    pairs = [(index, index ^ stride) for index in range(size)]
+    mine = lax.dynamic_index_in_dim(partial, digit, 0, keepdims=False)
+    other = lax.dynamic_index_in_dim(partial, 1 - digit, 0, keepdims=False)
+    return mine.astype(jnp.float32) + lax.ppermute(other.astype(link_dtype), axis_name, pairs).astype(jnp.float32)
+
+
+def row_reduce(partial, link_dtype):
+    count, rows, width = partial.shape
+    split = width // 2
+    first = partial[:, :, :split].reshape(4, 8, rows, split)
+    first = ring_reduce(first, "row", 8, link_dtype).reshape(2, 4, rows, split)
+    first = jnp.swapaxes(first, 0, 1)
+    first = ring_reduce(first, "row", 1, link_dtype)
+    second = partial[:, :, split:].reshape(4, 2, 4, rows, split)
+    second = jnp.transpose(second, (2, 0, 1, 3, 4))
+    second = ring_reduce(second, "row", 1, link_dtype).reshape(4, 2, rows, split)
+    second = ring_reduce(second, "row", 8, link_dtype)
+    both = jnp.concatenate([first, second], axis=-1)
+    return pair_reduce(both, "row", 4, link_dtype)
+
+
 def all_sum(terms):
     axes = ("row", "col")
     count = lax.axis_size("row") * lax.axis_size("col")
@@ -122,7 +178,7 @@
         values, coords[0], coords[1], live_count, row_source, col_tiles, True, jnp.bfloat16
     )
     back_partial = back_partial.reshape(n_row, sub_rows, width)
-    feature_grad = scatter_sum(back_partial, "row").reshape(1, 1, sub_rows, width)
+    feature_grad = row_reduce(back_partial, jnp.bfloat16).reshape(1, 1, sub_rows, width)
     return (activated.reshape(1, 1, sub_rows, width), feature_grad, weight_grad)
 
 

time: 435 us -> 413 us (0.949)
  Pallas kernels: 24.3 us -> 97.6 us
  blocking collectives: 108 us -> 50.2 us
  waiting for transfers between devices: 211 us -> 173 us
  starting transfers between devices: 61.7 us -> 52.1 us
  local copies, waits for them, and re-layouts: 5.81 us -> 13.7 us
    all_to_all x1, waiting for transfers between devices: 97.5 us -> 0.01 us  [all_sum(): lax.all_to_all(pieces, axes, 0, 0, tiled=True)]
    pallas_call x2, Pallas kernels: 24.3 us -> 97.6 us  [tile_aggregate(): pl.pallas_call(kernel, grid_spec=grid_spec, out_shape=jax.ShapeDtypeStruc...]
    all_to_all x1, starting transfers between devices: 53.2 us -> 15 us  [all_sum(): lax.all_to_all(pieces, axes, 0, 0, tiled=True)]
    ppermute x0 -> x17, waiting for transfers between devices: none -> 30.5 us  [the longest x4 14.7 us: ring_reduce(): from_right = lax.ppermute(to_left, axis_name, leftward)]
    all_to_all x1 -> x0, blocking collectives: 30.2 us -> none  [all_sum(): lax.all_to_all(pieces, axes, 0, 0, tiled=True)]
    all_gather x1, waiting for transfers between devices: 0.02 us -> 29.1 us  [shards(): lax.all_gather(own_grad.reshape(1, 1, sub_rows, width), 'col', axis=1, ti...]
    all_to_all x1, blocking collectives: 77.9 us -> 50.2 us  [scatter_sum(): received = lax.all_to_all(partial, axis_name, 0, 0, tiled=True)]
    ppermute x0 -> x17, starting transfers between devices: none -> 24.1 us  [the longest x4 7.5 us: ring_reduce(): relay_right = lax.ppermute(from_right[lead:], axis_name, leftward)]
  transfers between devices with their start and end apart: 4 -> 21, of which waited for: 2 -> 8; matrix products, arithmetic and copies ran while one was open for 1% -> 3% of each run, Pallas kernels for 3% -> 0%
where the time goes in v3:
time: 413 us; the launch traced here: 412 us
  waiting for transfers between devices  173 us (42%)
  Pallas kernels  97.6 us (24%)
  starting transfers between devices  52.1 us (13%)
  blocking collectives  50.2 us (12%)
  between operations  15.2 us (4%)
  local copies, waits for them, and re-layouts  13.7 us (3%)
  other arithmetic  7.65 us (2%)
    all_gather x1, waiting for transfers between devices, shards(): column_block = lax.all_gather(features, 'row', axis=1, tiled=True)  113 us
    pallas_call x2, Pallas kernels, tile_aggregate(): pl.pallas_call(kernel, grid_spec=grid_spec, out_shape=jax.ShapeDtypeStruc...  97.6 us
    all_to_all x1, blocking collectives, scatter_sum(): received = lax.all_to_all(partial, axis_name, 0, 0, tiled=True)  50.2 us
    all_gather x1, waiting for transfers between devices, shards(): lax.all_gather(own_grad.reshape(1, 1, sub_rows, width), 'col', axis=1, ti...  29.1 us
    all_to_all x1, starting transfers between devices, all_sum(): lax.all_to_all(pieces, axes, 0, 0, tiled=True)  15 us
    ppermute x4, waiting for transfers between devices, ring_reduce(): from_right = lax.ppermute(to_left, axis_name, leftward)  14.7 us
    all_to_all x1, starting transfers between devices, all_sum(): return lax.all_to_all(spread, axes, 0, 0, tiled=True).reshape(rows, width)  12.9 us
  transfers between devices with their start and end apart: 21, of which 8 were waited for; matrix products, arithmetic and copies ran while one was open for 3% of the time, Pallas kernels for 0%

profile of v3, /device:TPU:72, one launch (start us, length us, event | category | flops | bytes accessed | tf_op | source)
XLA Modules:
  0.0 411.5 jit_solution(17017662438703055285)
XLA Ops:
  7.2 0.7 all-gather.4.cloned.1.call-update
  7.9 0.0 all-gather.6.cloned.1.call-start
  8.6 0.8 fusion.27
  9.4 112.8 %all-gather.4.cloned.1.call-done = bf16[1,32,256,256]{3,2,0,1:T(8,128)(2,1)} async-done(((bf16[1,1,256,256]{3,2,0,1:T(8,128)(2,1)}), bf16[1,32,256,256]{3,2,0,1:T(8,128)(2,1)}) %all-gather.4.cloned.1.call-update) | async-done | bytes 4194320 | tf_op jit(solution)/shard_map/all_gather | solution.py:155
  122.2 43.5 %shard_map.85 = f32[16,128,256]{2,1,0:T(8,128)S(1)} custom-call(s32[256]{0:T(256)S(1)} %bitcast.109, s32[256]{0:T(256)S(1)} %bitcast.107, s32[1]{0:T(128)} %bitcast.102.count_ref, bf16[256,128,128]{2,1,0:T(8,128)(2,1)} %bitcast.111, bf16[64,128,256]{2,1,0:T(8,128)(2,1)} %bitcast.118), custom_call_target="tpu_custom_call" | custom-call | flops 2147483648 | bytes 14680064 | tf_op jit(solution)/shard_map/pallas_call | solution.py:60
  165.7 50.2 %all_to_all.15 = f32[8,256,256]{2,1,0:T(8,128)S(1)} all-to-all(f32[8,256,256]{2,1,0:T(8,128)S(1)} %bitcast.105), channel_id=1, replica_groups=mesh['row'=32,'col'=8] {'col'}, dimensions={0} | all-to-all | bytes 4194304 | tf_op jit(solution)/shard_map/all_to_all | solution.py:75
  215.9 0.1 reduce_sum.18
  216.0 0.8 copy-done.8
  216.8 0.9 fusion.11
  217.7 0.9 convolution_convert_fusion
  218.8 29.1 %all-gather.6.cloned.1.call-done = bf16[2048,256]{1,0:T(8,128)(2,1)} async-done(((bf16[256,256]{1,0:T(8,128)(2,1)}), bf16[2048,256]{1,0:T(8,128)(2,1)}) %all-gather.6.cloned.1.call-update) | async-done | bytes 1048592 | tf_op jit(solution)/shard_map/all_gather | solution.py:174
  247.9 1.2 copy-done.1
  249.1 54.1 %shard_map.86 = bf16[64,128,256]{2,1,0:T(8,128)(2,1)S(1)} custom-call(s32[256]{0:T(256)S(1)} %bitcast.108, s32[256]{0:T(256)S(1)} %bitcast.110, s32[1]{0:T(128)} %bitcast.103.count_ref, bf16[256,128,128]{2,1,0:T(8,128)(2,1)} %bitcast.112, bf16[16,128,256]{2,1,0:T(8,128)(2,1)S(1)} %bitcast.106), custom_call_target="tpu_custom_call" | custom-call | flops 2147483648 | bytes 13631488 | tf_op jit(solution)/shard_map/pallas_call | solution.py:60
  303.2 0.8 fusion.26
  304.0 0.1 dynamic-slice_bitcast_fusion.4
  304.1 0.1 pad_maximum_fusion.1
  304.2 1.1 copy-done.2
  305.3 0.1 pad_maximum_fusion
  305.4 2.1 collective-permute-start
  307.5 0.1 dynamic-slice_bitcast_fusion.2
  307.7 0.1 pad_maximum_fusion.3
  307.7 0.8 collective-permute-start.9
  308.5 1.0 pad_maximum_fusion.2
  309.5 1.3 collective-permute-start.8
  310.8 14.7 %collective-permute-done.1 = bf16[12,256,128]{2,1,0:T(8,128)(2,1)S(1)} collective-permute-done((bf16[12,256,128]{2,1,0:T(8,128)(2,1)S(1)}, bf16[12,256,128]{2,1,0:T(8,128)(2,1)S(1)}, u32[]{:S(2)}, u32[]{:S(2)}) %collective-permute-start.1) | collective-permute-done | bytes 786464 | tf_op jit(solution)/shard_map/ppermute | solution.py:103
  325.5 0.8 slice.156
  326.3 0.9 collective-permute-start.3
  327.2 0.8 slice.155
  328.0 0.2 copy-done.5
  328.3 1.1 collective-permute-start.2
  329.3 0.2 convolution_bitcast_fusion
  329.6 1.0 copy.16
  330.6 15.0 %all-to-all-start.1 = ((f32[256,1,256]{2,1,0:T(1,128)}), f32[256,1,256]{2,1,0:T(1,128)S(1)}, u32[]{:S(2)}, u32[]{:S(2)}) async-start(f32[256,1,256]{2,1,0:T(1,128)} %copy.16), calls=%async_computation.1 | async-start | bytes 524288 | tf_op jit(solution)/shard_map/all_to_all | solution.py:140
  345.6 1.0 slice.169
  346.5 0.6 collective-permute-start.11
  347.1 1.0 slice.168
  348.1 1.8 collective-permute-start.10
  349.9 1.8 fusion.3
  351.6 0.1 fusion.19
  351.8 1.5 collective-permute-start.5
  353.2 0.7 collective-permute-start.4
  354.0 3.8 collective-permute-done.11
  357.8 1.4 collective-permute-done.10
  359.1 1.4 fusion.1
  360.6 1.0 copy-done.3
  361.6 0.1 fusion.17
  361.7 2.5 collective-permute-start.13
  364.2 0.1 collective-permute-start.12
  364.3 0.7 copy-done.6
  364.9 3.2 collective-permute-start.7
  368.1 0.7 copy-done.7
  368.9 0.3 reduce_sum.19
  369.2 0.8 broadcast_in_dim.2
  370.0 12.9 %all-to-all-start.2 = ((f32[256,1,256]{2,1,0:T(1,128)}), f32[256,1,256]{2,1,0:T(1,128)S(1)}, u32[]{:S(2)}, u32[]{:S(2)}) async-start(f32[256,1,256]{2,1,0:T(1,128)} %broadcast_in_dim.2), calls=%async_computation.2 | async-start | bytes 524288 | tf_op jit(solution)/shard_map/all_to_all | solution.py:142
  382.9 2.8 collective-permute-start.15
  385.8 0.1 collective-permute-start.14
  385.9 1.0 fusion.15
  386.9 1.1 collective-permute-done.15
  388.0 3.5 collective-permute-done.14
  391.5 1.0 fusion.13
  392.5 4.7 %collective-permute-start.16 = (bf16[256,256]{1,0:T(8,128)(2,1)S(1)}, bf16[256,256]{1,0:T(8,128)(2,1)S(1)}, u32[]{:S(2)}, u32[]{:S(2)}) collective-permute-start(bf16[256,256]{1,0:T(8,128)(2,1)S(1)} %fusion.21), channel_id=1, source_target_pairs={{0,32},{8,40},{16,48},{24,56},{32,0},{40,8},{48,16},{56,24},{64,96... | collective-permute-start | bytes 393224 | tf_op jit(solution)/shard_map/ppermute | solution.py:117
  397.3 0.7 copy.22
  398.0 6.0 %collective-permute-done.16 = bf16[256,256]{1,0:T(8,128)(2,1)S(1)} collective-permute-done((bf16[256,256]{1,0:T(8,128)(2,1)S(1)}, bf16[256,256]{1,0:T(8,128)(2,1)S(1)}, u32[]{:S(2)}, u32[]{:S(2)}) %collective-permute-start.16) | collective-permute-done | bytes 131104 | tf_op jit(solution)/shard_map/ppermute | solution.py:117
  404.0 0.7 fusion.9
  (41 shorter events, 0.3 us)
Async XLA Ops:
  7.2 208.8 %copy-start = (bf16[256,256]{1,0:T(8,128)(2,1)S(1)}, bf16[256,256]{1,0:T(8,128)(2,1)}, u32[]{:S(2)}) copy-start(bf16[256,256]{1,0:T(8,128)(2,1)} %param.10) | copy-start | bytes 393220
  7.2 115.0 %all-gather.4.cloned.1.call-start = ((), (), s32[]{:S(2)}) async-start(), calls=%async_computation.3 | async-start | bytes 4325376 | tf_op jit(solution)/shard_map/all_gather | solution.py:155
  7.9 239.9 %all-gather.6.cloned.1.call-start = ((), (), s32[]{:S(2)}) async-start(), calls=%async_computation.4 | async-start | bytes 1179648 | tf_op jit(solution)/shard_map/all_gather | solution.py:174
  215.9 0.9 copy-start.8
  247.8 1.2 copy-start.1
  304.0 1.4 copy-start.2
  305.3 20.2 %collective-permute-start.1 = (bf16[12,256,128]{2,1,0:T(8,128)(2,1)S(1)}, bf16[12,256,128]{2,1,0:T(8,128)(2,1)S(1)}, u32[]{:S(2)}, u32[]{:S(2)}) collective-permute-start(bf16[12,256,128]{2,1,0:T(8,128)(2,1)S(1)} %pad_maximum_fusion.1), channel_id=1, source_target_pairs={{0,192},{8,200},{16,208},{24,216},{32,224},{40,232},{48,240},{56,2... | collective-permute-start | bytes 2359304 | tf_op jit(solution)/shard_map/ppermute | solution.py:103
  305.4 21.8 %collective-permute-start = (bf16[12,256,128]{2,1,0:T(8,128)(2,1)S(1)}, bf16[12,256,128]{2,1,0:T(8,128)(2,1)S(1)}, u32[]{:S(2)}, u32[]{:S(2)}) collective-permute-start(bf16[12,256,128]{2,1,0:T(8,128)(2,1)S(1)} %pad_maximum_fusion), channel_id=1, source_target_pairs={{0,64},{8,72},{16,80},{24,88},{32,96},{40,104},{48,112},{56,120},{... | collective-permute-start | bytes 2359304 | tf_op jit(solution)/shard_map/ppermute | solution.py:102
  307.7 37.8 %collective-permute-start.9 = (bf16[6,2,256,128]{3,2,1,0:T(8,128)(2,1)S(1)}, bf16[6,2,256,128]{3,2,1,0:T(8,128)(2,1)}, u32[]{:S(2)}, u32[]{:S(2)}) collective-permute-start(bf16[6,2,256,128]{3,2,1,0:T(8,128)(2,1)S(1)} %pad_maximum_fusion.3), channel_id=1, source_target_pairs={{0,24},{8,0},{16,8},{24,16},{32,56},{40,32},{48,40},{56,48},{64,88... | collective-permute-start | bytes 2359304 | tf_op jit(solution)/shard_map/ppermute | solution.py:103
  309.5 37.6 %collective-permute-start.8 = (bf16[6,2,256,128]{3,2,1,0:T(8,128)(2,1)}, bf16[6,2,256,128]{3,2,1,0:T(8,128)(2,1)}, u32[]{:S(2)}, u32[]{:S(2)}) collective-permute-start(bf16[6,2,256,128]{3,2,1,0:T(8,128)(2,1)} %pad_maximum_fusion.2), channel_id=1, source_target_pairs={{0,8},{8,16},{16,24},{24,0},{32,40},{40,48},{48,56},{56,32},{64,72... | collective-permute-start | bytes 2359304 | tf_op jit(solution)/shard_map/ppermute | solution.py:102
  325.5 1.7 copy-start.4
  326.3 23.6 %collective-permute-start.3 = (bf16[4,256,128]{2,1,0:T(8,128)(2,1)}, bf16[4,256,128]{2,1,0:T(8,128)(2,1)}, u32[]{:S(2)}, u32[]{:S(2)}) collective-permute-start(bf16[4,256,128]{2,1,0:T(8,128)(2,1)} %slice.156), channel_id=1, source_target_pairs={{0,192},{8,200},{16,208},{24,216},{32,224},{40,232},{48,240},{56,2... | collective-permute-start | bytes 786440 | tf_op jit(solution)/shard_map/ppermute | solution.py:105
  327.2 1.0 copy-start.5
  328.3 21.6 %collective-permute-start.2 = (bf16[4,256,128]{2,1,0:T(8,128)(2,1)}, bf16[4,256,128]{2,1,0:T(8,128)(2,1)}, u32[]{:S(2)}, u32[]{:S(2)}) collective-permute-start(bf16[4,256,128]{2,1,0:T(8,128)(2,1)} %slice.155), channel_id=1, source_target_pairs={{0,64},{8,72},{16,80},{24,88},{32,96},{40,104},{48,112},{56,120},{... | collective-permute-start | bytes 786440 | tf_op jit(solution)/shard_map/ppermute | solution.py:104
  330.6 38.3 %all-to-all-start.1 = ((f32[256,1,256]{2,1,0:T(1,128)}), f32[256,1,256]{2,1,0:T(1,128)S(1)}, u32[]{:S(2)}, u32[]{:S(2)}) async-start(f32[256,1,256]{2,1,0:T(1,128)} %copy.16), calls=%async_computation.1 | async-start | bytes 524288 | tf_op jit(solution)/shard_map/all_to_all | solution.py:140
  346.5 11.2 %collective-permute-start.11 = (bf16[2,2,256,128]{3,2,1,0:T(8,128)(2,1)S(1)}, bf16[2,2,256,128]{3,2,1,0:T(8,128)(2,1)S(1)}, u32[]{:S(2)}, u32[]{:S(2)}) collective-permute-start(bf16[2,2,256,128]{3,2,1,0:T(8,128)(2,1)S(1)} %slice.169), channel_id=1, source_target_pairs={{0,24},{8,0},{16,8},{24,16},{32,56},{40,32},{48,40},{56,48},{64,88... | collective-permute-start | bytes 786440 | tf_op jit(solution)/shard_map/ppermute | solution.py:105
  348.1 11.0 %collective-permute-start.10 = (bf16[2,2,256,128]{3,2,1,0:T(8,128)(2,1)S(1)}, bf16[2,2,256,128]{3,2,1,0:T(8,128)(2,1)S(1)}, u32[]{:S(2)}, u32[]{:S(2)}) collective-permute-start(bf16[2,2,256,128]{3,2,1,0:T(8,128)(2,1)S(1)} %slice.168), channel_id=1, source_target_pairs={{0,8},{8,16},{16,24},{24,0},{32,40},{40,48},{48,56},{56,32},{64,72... | collective-permute-start | bytes 786440 | tf_op jit(solution)/shard_map/ppermute | solution.py:104
  351.8 12.5 %collective-permute-start.5 = (bf16[3,256,128]{2,1,0:T(8,128)(2,1)S(1)}, bf16[3,256,128]{2,1,0:T(8,128)(2,1)S(1)}, u32[]{:S(2)}, u32[]{:S(2)}) collective-permute-start(bf16[3,256,128]{2,1,0:T(8,128)(2,1)S(1)} %pad_maximum_fusion.5), channel_id=1, source_target_pairs={{0,24},{8,0},{16,8},{24,16},{32,56},{40,32},{48,40},{56,48},{64,88... | collective-permute-start | bytes 589832 | tf_op jit(solution)/shard_map/ppermute | solution.py:103
  353.2 14.9 %collective-permute-start.4 = (bf16[3,256,128]{2,1,0:T(8,128)(2,1)S(1)}, bf16[3,256,128]{2,1,0:T(8,128)(2,1)S(1)}, u32[]{:S(2)}, u32[]{:S(2)}) collective-permute-start(bf16[3,256,128]{2,1,0:T(8,128)(2,1)S(1)} %pad_maximum_fusion.4), channel_id=1, source_target_pairs={{0,8},{8,16},{16,24},{24,0},{32,40},{40,48},{48,56},{56,32},{64,72... | collective-permute-start | bytes 589832 | tf_op jit(solution)/shard_map/ppermute | solution.py:102
  360.6 1.0 copy-start.3
  361.7 21.3 %collective-permute-start.13 = (bf16[3,256,128]{2,1,0:T(8,128)(2,1)S(1)}, bf16[3,256,128]{2,1,0:T(8,128)(2,1)S(1)}, u32[]{:S(2)}, u32[]{:S(2)}) collective-permute-start(bf16[3,256,128]{2,1,0:T(8,128)(2,1)S(1)} %pad_maximum_fusion.7), channel_id=1, source_target_pairs={{0,192},{8,200},{16,208},{24,216},{32,224},{40,232},{48,240},{56,2... | collective-permute-start | bytes 589832 | tf_op jit(solution)/shard_map/ppermute | solution.py:103
  364.2 21.6 %collective-permute-start.12 = (bf16[3,256,128]{2,1,0:T(8,128)(2,1)S(1)}, bf16[3,256,128]{2,1,0:T(8,128)(2,1)S(1)}, u32[]{:S(2)}, u32[]{:S(2)}) collective-permute-start(bf16[3,256,128]{2,1,0:T(8,128)(2,1)S(1)} %pad_maximum_fusion.6), channel_id=1, source_target_pairs={{0,64},{8,72},{16,80},{24,88},{32,96},{40,104},{48,112},{56,120},{... | collective-permute-start | bytes 589832 | tf_op jit(solution)/shard_map/ppermute | solution.py:102
  364.3 0.7 copy-start.6
  364.9 20.9 %collective-permute-start.7 = (bf16[1,256,128]{2,1,0:T(8,128)(2,1)S(1)}, bf16[1,256,128]{2,1,0:T(8,128)(2,1)S(1)}, u32[]{:S(2)}, u32[]{:S(2)}) collective-permute-start(bf16[1,256,128]{2,1,0:T(8,128)(2,1)S(1)} %slice.162), channel_id=1, source_target_pairs={{0,24},{8,0},{16,8},{24,16},{32,56},{40,32},{48,40},{56,48},{64,88... | collective-permute-start | bytes 196616 | tf_op jit(solution)/shard_map/ppermute | solution.py:105
  368.1 0.7 copy-start.7
  368.8 17.0 %collective-permute-start.6 = (bf16[1,256,128]{2,1,0:T(8,128)(2,1)S(1)}, bf16[1,256,128]{2,1,0:T(8,128)(2,1)S(1)}, u32[]{:S(2)}, u32[]{:S(2)}) collective-permute-start(bf16[1,256,128]{2,1,0:T(8,128)(2,1)S(1)} %slice.161), channel_id=1, source_target_pairs={{0,8},{8,16},{16,24},{24,0},{32,40},{40,48},{48,56},{56,32},{64,72... | collective-permute-start | bytes 196616 | tf_op jit(solution)/shard_map/ppermute | solution.py:104
  370.0 27.3 %all-to-all-start.2 = ((f32[256,1,256]{2,1,0:T(1,128)}), f32[256,1,256]{2,1,0:T(1,128)S(1)}, u32[]{:S(2)}, u32[]{:S(2)}) async-start(f32[256,1,256]{2,1,0:T(1,128)} %broadcast_in_dim.2), calls=%async_computation.2 | async-start | bytes 524288 | tf_op jit(solution)/shard_map/all_to_all | solution.py:142
  382.9 5.0 %collective-permute-start.15 = (bf16[1,256,128]{2,1,0:T(8,128)(2,1)S(1)}, bf16[1,256,128]{2,1,0:T(8,128)(2,1)S(1)}, u32[]{:S(2)}, u32[]{:S(2)}) collective-permute-start(bf16[1,256,128]{2,1,0:T(8,128)(2,1)S(1)} %slice.175), channel_id=1, source_target_pairs={{0,192},{8,200},{16,208},{24,216},{32,224},{40,232},{48,240},{56,2... | collective-permute-start | bytes 196616 | tf_op jit(solution)/shard_map/ppermute | solution.py:105
  385.8 5.8 %collective-permute-start.14 = (bf16[1,256,128]{2,1,0:T(8,128)(2,1)S(1)}, bf16[1,256,128]{2,1,0:T(8,128)(2,1)S(1)}, u32[]{:S(2)}, u32[]{:S(2)}) collective-permute-start(bf16[1,256,128]{2,1,0:T(8,128)(2,1)S(1)} %slice.174), channel_id=1, source_target_pairs={{0,64},{8,72},{16,80},{24,88},{32,96},{40,104},{48,112},{56,120},{... | collective-permute-start | bytes 196616 | tf_op jit(solution)/shard_map/ppermute | solution.py:104
  392.5 11.4 %collective-permute-start.16 = (bf16[256,256]{1,0:T(8,128)(2,1)S(1)}, bf16[256,256]{1,0:T(8,128)(2,1)S(1)}, u32[]{:S(2)}, u32[]{:S(2)}) collective-permute-start(bf16[256,256]{1,0:T(8,128)(2,1)S(1)} %fusion.21), channel_id=1, source_target_pairs={{0,32},{8,40},{16,48},{24,56},{32,0},{40,8},{48,16},{56,24},{64,96... | collective-permute-start | bytes 393224 | tf_op jit(solution)/shard_map/ppermute | solution.py:117
Sparse Core Ops, SparseCore 0:
  11.5 110.6 all-gather.3
  218.7 29.0 all-gather.5

commit v4 on v3

--- a/solution.py
+++ b/solution.py
@@ -117,6 +117,72 @@
     return mine.astype(jnp.float32) + lax.ppermute(other.astype(link_dtype), axis_name, pairs).astype(jnp.float32)
 
 
+def digit_of(axis_name, stride, digits):
+    return (lax.axis_index(axis_name) // stride) % digits
+
+
+def pair_gather(block, axis_name, stride):
+    size = lax.axis_size(axis_name)
+    other = lax.ppermute(block, axis_name, [(index, index ^ stride) for index in range(size)])
+    first = digit_of(axis_name, stride, 2) == 0
+    return jnp.stack([jnp.where(first, block, other), jnp.where(first, other, block)])
+
+
+def ring_gather(block, axis_name, stride):
+    size = lax.axis_size(axis_name)
+    rightward = ring_step_pairs(size, stride, 4, 1)
+    leftward = ring_step_pairs(size, stride, 4, -1)
+    half = block.shape[0] // 2
+    from_left = lax.ppermute(block, axis_name, rightward)
+    from_right = lax.ppermute(block, axis_name, leftward)
+    far_low = lax.ppermute(from_left[:half], axis_name, rightward)
+    far_high = lax.ppermute(from_right[half:], axis_name, leftward)
+    far = jnp.concatenate([far_low, far_high])
+    by_offset = jnp.stack([block, from_right, far, from_left])
+    return jnp.roll(by_offset, digit_of(axis_name, stride, 4), axis=0)
+
+
+def line_gather(block, axis_name, stride):
+    size = lax.axis_size(axis_name)
+    parts = [block]
+    for shift in (3, 2, 1):
+        parts.append(lax.ppermute(block, axis_name, ring_step_pairs(size, stride, 4, shift)))
+    return jnp.roll(jnp.stack(parts), digit_of(axis_name, stride, 4), axis=0)
+
+
+def line_reduce(partial, axis_name, stride, link_dtype):
+    size = lax.axis_size(axis_name)
+    digit = digit_of(axis_name, stride, 4)
+    total = lax.dynamic_index_in_dim(partial, digit, 0, keepdims=False).astype(jnp.float32)
+    for shift in (1, 2, 3):
+        outgoing = lax.dynamic_index_in_dim(partial, (digit + shift) % 4, 0, keepdims=False)
+        incoming = lax.ppermute(outgoing.astype(link_dtype), axis_name, ring_step_pairs(size, stride, 4, shift))
+        total = total + incoming.astype(jnp.float32)
+    return total
+
+
+def row_gather(block):
+    pair = pair_gather(block, "row", 4)
+    plane = jnp.swapaxes(ring_gather(pair, "row", 1), 0, 1)
+    plane = plane.reshape((8,) + block.shape)
+    return ring_gather(plane, "row", 8).reshape((32,) + block.shape)
+
+
+def col_gather(block):
+    pair = pair_gather(block, "col", 1)
+    return line_gather(pair, "col", 2).reshape((8,) + block.shape)
+
+
+def col_reduce(partial, link_dtype):
+    core = digit_of("col", 1, 2)
+    size = lax.axis_size("col")
+    split = partial.reshape((4, 2) + partial.shape[1:])
+    mine = lax.dynamic_index_in_dim(split, core, 1, keepdims=False).astype(jnp.float32)
+    other = lax.dynamic_index_in_dim(split, 1 - core, 1, keepdims=False).astype(link_dtype)
+    swapped = lax.ppermute(other, "col", [(index, index ^ 1) for index in range(size)])
+    return line_reduce(mine + swapped.astype(jnp.float32), "col", 2, link_dtype)
+
+
 def row_reduce(partial, link_dtype):
     count, rows, width = partial.shape
     split = width // 2
@@ -152,14 +218,14 @@
     n_col = lax.axis_size("col")
     n_row = lax.axis_size("row")
     row_tiles = n_col * sub_rows // tile_side
-    column_block = lax.all_gather(features, "row", axis=1, tiled=True)
+    column_block = row_gather(features.reshape(sub_rows, width))
     col_source = column_block.reshape(-1, tile_side, width)
     col_tiles = col_source.shape[0]
     partial_value = tile_aggregate(
         values, coords[1], coords[0], live_count, col_source, row_tiles, False, jnp.float32
     )
     partial_value = partial_value.reshape(n_col, sub_rows, width)
-    share = scatter_sum(partial_value, "col")
+    share = col_reduce(partial_value, jnp.float32)
     mixed = share.astype(jnp.bfloat16).reshape(sub_rows, width)
     pre = jnp.dot(mixed, weight_matrix, preferred_element_type=jnp.float32)
     sigma = jax.nn.sigmoid(pre)
@@ -171,7 +237,7 @@
     own_grad = jnp.dot(pre_grad, weight_matrix.T, preferred_element_type=jnp.float32).astype(
         jnp.bfloat16
     )
-    mixed_grad = lax.all_gather(own_grad.reshape(1, 1, sub_rows, width), "col", axis=1, tiled=True)
+    mixed_grad = col_gather(own_grad)
     weight_grad = all_sum(weight_terms)
     row_source = mixed_grad.reshape(row_tiles, tile_side, width)
     back_partial = tile_aggregate(

time: 413 us -> 337 us (0.82); the launches traced: 412 us -> 330 us
  starting transfers between devices: 52.1 us -> 166 us
  Pallas kernels: 97.6 us -> 24.3 us
  waiting for transfers between devices: 173 us -> 106 us
  blocking collectives: 50.2 us -> 0 us
  between operations: 15.2 us -> 2.03 us
  other arithmetic: 7.65 us -> 15.2 us
    all_gather x2 -> x0, waiting for transfers between devices: 142 us -> none  [the longest x1 113 us: shards(): column_block = lax.all_gather(features, 'row', axis=1, tiled=True)]
    ppermute x0 -> x17, waiting for transfers between devices: none -> 89 us  [the longest x2 25.7 us: ring_gather(): from_left = lax.ppermute(block, axis_name, rightward)]
    pallas_call x2, Pallas kernels: 97.6 us -> 24.3 us  [tile_aggregate(): pl.pallas_call(kernel, grid_spec=grid_spec, out_shape=jax.ShapeDtypeStruc...]
    all_to_all x1 -> x0, blocking collectives: 50.2 us -> none  [scatter_sum(): received = lax.all_to_all(partial, axis_name, 0, 0, tiled=True)]
    ppermute x0 -> x17, starting transfers between devices: none -> 35.6 us  [the longest x3 14.9 us: line_reduce(): lax.ppermute(outgoing.astype(link_dtype), axis_name, ring_step_pairs(size...]
    all_to_all x1, starting transfers between devices: 15 us -> 45.9 us  [all_sum(): lax.all_to_all(pieces, axes, 0, 0, tiled=True)]
    ppermute x4, starting transfers between devices: 4.24 us -> 27.2 us  [ring_reduce(): from_left = lax.ppermute(to_right, axis_name, rightward)]
    ppermute x4, starting transfers between devices: 4.7 us -> 19.8 us  [ring_reduce(): from_right = lax.ppermute(to_left, axis_name, leftward)]
  transfers between devices with their start and end apart: 21 -> 36, of which waited for: 8 -> 20; matrix products, arithmetic and copies ran while one was open for 3% -> 5% of each run, Pallas kernels for 0% -> 0%
where the time goes in v4:
time: 337 us; the launch traced here: 330 us
  starting transfers between devices  166 us (49%)
  waiting for transfers between devices  106 us (31%)
  Pallas kernels  24.3 us (7%)
  local copies, waits for them, and re-layouts  15.9 us (5%)
  other arithmetic  15.2 us (5%)
    all_to_all x1, starting transfers between devices, all_sum(): lax.all_to_all(pieces, axes, 0, 0, tiled=True)  45.9 us
    ppermute x4, starting transfers between devices, ring_reduce(): from_left = lax.ppermute(to_right, axis_name, rightward)  27.2 us
    ppermute x2, waiting for transfers between devices, ring_gather(): from_left = lax.ppermute(block, axis_name, rightward)  25.7 us
    pallas_call x2, Pallas kernels, tile_aggregate(): pl.pallas_call(kernel, grid_spec=grid_spec, out_shape=jax.ShapeDtypeStruc...  24.3 us
    ppermute x3, waiting for transfers between devices, line_gather(): lax.ppermute(block, axis_name, ring_step_pairs(size, stride, 4, shift))  21.2 us
    ppermute x4, starting transfers between devices, ring_reduce(): from_right = lax.ppermute(to_left, axis_name, leftward)  19.8 us
    ppermute x3, waiting for transfers between devices, line_reduce(): lax.ppermute(outgoing.astype(link_dtype), axis_name, ring_step_pairs(size...  19.7 us
    ppermute x4, starting transfers between devices, ring_reduce(): relay_right = lax.ppermute(from_right[lead:], axis_name, leftward)  16.1 us
  transfers between devices with their start and end apart: 36, of which 20 were waited for; matrix products, arithmetic and copies ran while one was open for 5% of the time, Pallas kernels for 0%

profile of v4, /device:TPU:72, one launch (start us, length us, event | category | flops | bytes accessed | tf_op | source)
XLA Modules:
  0.0 330.5 jit_solution(9462139233554411368)
XLA Ops:
  0.6 5.5 %collective-permute-start = (bf16[256,256]{1,0:T(8,128)(2,1)}, bf16[256,256]{1,0:T(8,128)(2,1)S(1)}, u32[]{:S(2)}, u32[]{:S(2)}) collective-permute-start(bf16[256,256]{1,0:T(8,128)(2,1)} %bitcast.194), channel_id=1, source_target_pairs={{0,32},{8,40},{16,48},{24,56},{32,0},{40,8},{48,16},{56,24},{64,96... | collective-permute-start | bytes 393224 | tf_op jit(solution)/shard_map/ppermute | solution.py:126
  6.1 6.9 %collective-permute-done = bf16[256,256]{1,0:T(8,128)(2,1)S(1)} collective-permute-done((bf16[256,256]{1,0:T(8,128)(2,1)}, bf16[256,256]{1,0:T(8,128)(2,1)S(1)}, u32[]{:S(2)}, u32[]{:S(2)}) %collective-permute-start) | collective-permute-done | bytes 131104 | tf_op jit(solution)/shard_map/ppermute | solution.py:126
  13.0 0.9 select_bitcast_fusion.3
  14.0 1.7 collective-permute-start.2
  16.1 5.4 %collective-permute-done.2 = bf16[2,256,256]{2,1,0:T(8,128)(2,1)S(1)} collective-permute-done((bf16[2,256,256]{2,1,0:T(8,128)(2,1)S(1)}, bf16[2,256,256]{2,1,0:T(8,128)(2,1)S(1)}, u32[]{:S(2)}, u32[]{:S(2)}) %collective-permute-start.2) | collective-permute-done | bytes 262176 | tf_op jit(solution)/shard_map/ppermute | solution.py:136
  21.6 1.7 collective-permute-start.3
  23.8 2.8 collective-permute-done.3
  26.6 1.7 collective-permute-done.4
  28.3 1.3 fusion.10
  29.6 1.6 collective-permute-start.6
  31.1 1.7 collective-permute-start.5
  32.9 20.3 %collective-permute-done.6 = bf16[8,256,256]{2,1,0:T(8,128)(2,1)S(1)} collective-permute-done((bf16[8,256,256]{2,1,0:T(8,128)(2,1)S(1)}, bf16[8,256,256]{2,1,0:T(8,128)(2,1)S(1)}, u32[]{:S(2)}, u32[]{:S(2)}) %collective-permute-start.6) | collective-permute-done | bytes 1048608 | tf_op jit(solution)/shard_map/ppermute | solution.py:136
  54.3 0.8 slice.171
  55.1 3.0 collective-permute-start.8
  58.9 6.8 %collective-permute-done.7 = bf16[4,256,256]{2,1,0:T(8,128)(2,1)} collective-permute-done((bf16[4,256,256]{2,1,0:T(8,128)(2,1)}, bf16[4,256,256]{2,1,0:T(8,128)(2,1)}, u32[]{:S(2)}, u32[]{:S(2)}) %collective-permute-start.7) | collective-permute-done | bytes 524320 | tf_op jit(solution)/shard_map/ppermute | solution.py:138
  65.9 1.3 fusion.18
  67.4 1.3 fusion.19
  68.7 2.3 constant_dynamic-slice_fusion
  71.0 11.8 %shard_map.85 = f32[16,128,256]{2,1,0:T(8,128)S(1)} custom-call(s32[256]{0:T(256)S(1)} %bitcast.172, s32[256]{0:T(256)S(1)} %bitcast.170, s32[1]{0:T(128)} %bitcast.164.count_ref, bf16[256,128,128]{2,1,0:T(8,128)(2,1)} %bitcast.174, bf16[64,128,256]{2,1,0:T(8,128)(2,1)} %bitcast.176), custom_call_target="tpu_custom_call" | custom-call | flops 2147483648 | bytes 14680064 | tf_op jit(solution)/shard_map/pallas_call | solution.py:60
  83.1 2.7 collective-permute-done.9
  85.8 1.5 bitcast_add_fusion
  87.3 3.1 collective-permute-start.10
  90.4 8.8 %collective-permute-start.11 = (f32[256,256]{1,0:T(8,128)S(1)}, f32[256,256]{1,0:T(8,128)S(1)}, u32[]{:S(2)}, u32[]{:S(2)}) collective-permute-start(f32[256,256]{1,0:T(8,128)S(1)} %get-tuple-element.21), channel_id=1, source_target_pairs={{0,4},{1,5},{2,6},{3,7},{4,0},{5,1},{6,2},{7,3},{8,12},{9,13},{10,... | collective-permute-start | bytes 786440 | tf_op jit(solution)/shard_map/ppermute | solution.py:159
  99.2 3.1 collective-permute-start.12
  102.3 14.9 %collective-permute-done.11 = f32[256,256]{1,0:T(8,128)S(1)} collective-permute-done((f32[256,256]{1,0:T(8,128)S(1)}, f32[256,256]{1,0:T(8,128)S(1)}, u32[]{:S(2)}, u32[]{:S(2)}) %collective-permute-start.11) | collective-permute-done | bytes 262176 | tf_op jit(solution)/shard_map/ppermute | solution.py:159
  117.2 4.8 %collective-permute-done.12 = f32[256,256]{1,0:T(8,128)S(1)} collective-permute-done((f32[256,256]{1,0:T(8,128)S(1)}, f32[256,256]{1,0:T(8,128)S(1)}, u32[]{:S(2)}, u32[]{:S(2)}) %collective-permute-start.12) | collective-permute-done | bytes 262176 | tf_op jit(solution)/shard_map/ppermute | solution.py:159
  122.0 0.9 fusion.27
  123.3 1.3 collective-permute-done.13
  124.7 2.6 collective-permute-start.14
  127.3 1.6 collective-permute-start.16
  128.8 16.4 %collective-permute-done.14 = bf16[2,256,256]{2,1,0:T(8,128)(2,1)S(1)} collective-permute-done((bf16[2,256,256]{2,1,0:T(8,128)(2,1)S(1)}, bf16[2,256,256]{2,1,0:T(8,128)(2,1)S(1)}, u32[]{:S(2)}, u32[]{:S(2)}) %collective-permute-start.14) | collective-permute-done | bytes 262176 | tf_op jit(solution)/shard_map/ppermute | solution.py:149
  145.2 4.8 %collective-permute-done.15 = bf16[2,256,256]{2,1,0:T(8,128)(2,1)S(1)} collective-permute-done((bf16[2,256,256]{2,1,0:T(8,128)(2,1)S(1)}, bf16[2,256,256]{2,1,0:T(8,128)(2,1)S(1)}, u32[]{:S(2)}, u32[]{:S(2)}) %collective-permute-start.15) | collective-permute-done | bytes 262176 | tf_op jit(solution)/shard_map/ppermute | solution.py:149
  150.0 1.2 fusion.3
  151.2 12.5 %shard_map.86 = bf16[64,128,256]{2,1,0:T(8,128)(2,1)S(1)} custom-call(s32[256]{0:T(256)S(1)} %bitcast.171, s32[256]{0:T(256)S(1)} %bitcast.173, s32[1]{0:T(128)} %bitcast.165.count_ref, bf16[256,128,128]{2,1,0:T(8,128)(2,1)} %bitcast.175, bf16[16,128,256]{2,1,0:T(8,128)(2,1)S(1)} %bitcast.169), custom_call_target="tpu_custom_call" | custom-call | flops 2147483648 | bytes 13631488 | tf_op jit(solution)/shard_map/pallas_call | solution.py:60
  164.8 1.2 copy-done.2
  166.0 25.1 %collective-permute-start.25 = (bf16[6,2,256,128]{3,2,1,0:T(8,128)(2,1)S(1)}, bf16[6,2,256,128]{3,2,1,0:T(8,128)(2,1)S(1)}, u32[]{:S(2)}, u32[]{:S(2)}) collective-permute-start(bf16[6,2,256,128]{3,2,1,0:T(8,128)(2,1)S(1)} %pad_maximum_fusion.2), channel_id=1, source_target_pairs={{0,8},{8,16},{16,24},{24,0},{32,40},{40,48},{48,56},{56,32},{64,72... | collective-permute-start | bytes 2359304 | tf_op jit(solution)/shard_map/ppermute | solution.py:102
  191.2 13.0 %collective-permute-start.26 = (bf16[6,2,256,128]{3,2,1,0:T(8,128)(2,1)S(1)}, bf16[6,2,256,128]{3,2,1,0:T(8,128)(2,1)S(1)}, u32[]{:S(2)}, u32[]{:S(2)}) collective-permute-start(bf16[6,2,256,128]{3,2,1,0:T(8,128)(2,1)S(1)} %pad_maximum_fusion.3), channel_id=1, source_target_pairs={{0,24},{8,0},{16,8},{24,16},{32,56},{40,32},{48,40},{56,48},{64,88... | collective-permute-start | bytes 2359304 | tf_op jit(solution)/shard_map/ppermute | solution.py:103
  204.5 1.0 pad_maximum_fusion.1
  205.4 3.2 collective-permute-start.18
  208.6 5.3 %collective-permute-done.25 = bf16[6,2,256,128]{3,2,1,0:T(8,128)(2,1)S(1)} collective-permute-done((bf16[6,2,256,128]{3,2,1,0:T(8,128)(2,1)S(1)}, bf16[6,2,256,128]{3,2,1,0:T(8,128)(2,1)S(1)}, u32[]{:S(2)}, u32[]{:S(2)}) %collective-permute-start.25) | collective-permute-done | bytes 786464 | tf_op jit(solution)/shard_map/ppermute | solution.py:102
  216.0 12.0 %collective-permute-start.28 = (bf16[2,2,256,128]{3,2,1,0:T(8,128)(2,1)}, bf16[2,2,256,128]{3,2,1,0:T(8,128)(2,1)}, u32[]{:S(2)}, u32[]{:S(2)}) collective-permute-start(bf16[2,2,256,128]{3,2,1,0:T(8,128)(2,1)} %slice.189), channel_id=1, source_target_pairs={{0,24},{8,0},{16,8},{24,16},{32,56},{40,32},{48,40},{56,48},{64,88... | collective-permute-start | bytes 786440 | tf_op jit(solution)/shard_map/ppermute | solution.py:105
  228.2 1.0 copy.21
  229.2 45.9 %all-to-all-start = ((f32[256,1,256]{2,1,0:T(1,128)}), f32[256,1,256]{2,1,0:T(1,128)S(1)}, u32[]{:S(2)}, u32[]{:S(2)}) async-start(f32[256,1,256]{2,1,0:T(1,128)} %copy.21), calls=%async_computation | async-start | bytes 524288 | tf_op jit(solution)/shard_map/all_to_all | solution.py:206
  275.1 1.0 slice.175
  276.1 1.6 collective-permute-start.19
  277.6 1.0 slice.176
  278.6 1.8 collective-permute-start.20
  280.5 1.8 fusion.15
  282.7 3.0 collective-permute-start.30
  285.8 2.2 collective-permute-done.19
  288.5 1.5 fusion.17
  290.0 1.0 copy-done.3
  291.1 1.6 collective-permute-start.21
  294.0 1.5 collective-permute-start.31
  296.2 1.7 collective-permute-start.32
  298.2 0.8 broadcast_in_dim.2
  299.1 11.7 %all-to-all-start.1 = ((f32[256,1,256]{2,1,0:T(1,128)}), f32[256,1,256]{2,1,0:T(1,128)S(1)}, u32[]{:S(2)}, u32[]{:S(2)}) async-start(f32[256,1,256]{2,1,0:T(1,128)} %broadcast_in_dim.2), calls=%async_computation.1 | async-start | bytes 524288 | tf_op jit(solution)/shard_map/all_to_all | solution.py:208
  310.8 1.6 collective-permute-start.23
  313.0 1.0 fusion.29
  314.0 1.8 collective-permute-done.23
  315.8 1.3 collective-permute-done.24
  317.1 1.0 fusion.31
  318.2 5.1 %collective-permute-start.33 = (bf16[256,256]{1,0:T(8,128)(2,1)S(1)}, bf16[256,256]{1,0:T(8,128)(2,1)S(1)}, u32[]{:S(2)}, u32[]{:S(2)}) collective-permute-start(bf16[256,256]{1,0:T(8,128)(2,1)S(1)} %fusion.40), channel_id=1, source_target_pairs={{0,32},{8,40},{16,48},{24,56},{32,0},{40,8},{48,16},{56,24},{64,96... | collective-permute-start | bytes 393224 | tf_op jit(solution)/shard_map/ppermute | solution.py:117
  324.7 4.8 %collective-permute-done.33 = bf16[256,256]{1,0:T(8,128)(2,1)S(1)} collective-permute-done((bf16[256,256]{1,0:T(8,128)(2,1)S(1)}, bf16[256,256]{1,0:T(8,128)(2,1)S(1)}, u32[]{:S(2)}, u32[]{:S(2)}) %collective-permute-start.33) | collective-permute-done | bytes 131104 | tf_op jit(solution)/shard_map/ppermute | solution.py:117
  (93 shorter events, 13.2 us)
Async XLA Ops:
  0.6 121.4 %copy-start = (bf16[256,256]{1,0:T(8,128)(2,1)S(1)}, bf16[256,256]{1,0:T(8,128)(2,1)}, u32[]{:S(2)}) copy-start(bf16[256,256]{1,0:T(8,128)(2,1)} %param.12) | copy-start | bytes 393220
  0.6 12.4 %collective-permute-start = (bf16[256,256]{1,0:T(8,128)(2,1)}, bf16[256,256]{1,0:T(8,128)(2,1)S(1)}, u32[]{:S(2)}, u32[]{:S(2)}) collective-permute-start(bf16[256,256]{1,0:T(8,128)(2,1)} %bitcast.194), channel_id=1, source_target_pairs={{0,32},{8,40},{16,48},{24,56},{32,0},{40,8},{48,16},{56,24},{64,96... | collective-permute-start | bytes 393224 | tf_op jit(solution)/shard_map/ppermute | solution.py:126
  14.0 7.5 %collective-permute-start.2 = (bf16[2,256,256]{2,1,0:T(8,128)(2,1)S(1)}, bf16[2,256,256]{2,1,0:T(8,128)(2,1)S(1)}, u32[]{:S(2)}, u32[]{:S(2)}) collective-permute-start(bf16[2,256,256]{2,1,0:T(8,128)(2,1)S(1)} %get-tuple-element.30), channel_id=1, source_target_pairs={{0,8},{8,16},{16,24},{24,0},{32,40},{40,48},{48,56},{56,32},{64,72... | collective-permute-start | bytes 786440 | tf_op jit(solution)/shard_map/ppermute | solution.py:136
  15.7 7.5 %collective-permute-start.1 = (bf16[2,256,256]{2,1,0:T(8,128)(2,1)S(1)}, bf16[2,256,256]{2,1,0:T(8,128)(2,1)S(1)}, u32[]{:S(2)}, u32[]{:S(2)}) collective-permute-start(bf16[2,256,256]{2,1,0:T(8,128)(2,1)S(1)} %get-tuple-element.30), channel_id=1, source_target_pairs={{0,24},{8,0},{16,8},{24,16},{32,56},{40,32},{48,40},{56,48},{64,88... | collective-permute-start | bytes 786440 | tf_op jit(solution)/shard_map/ppermute | solution.py:137
  21.6 5.0 %collective-permute-start.3 = (bf16[1,256,256]{2,1,0:T(8,128)(2,1)S(1)}, bf16[1,256,256]{2,1,0:T(8,128)(2,1)S(1)}, u32[]{:S(2)}, u32[]{:S(2)}) collective-permute-start(bf16[1,256,256]{2,1,0:T(8,128)(2,1)S(1)} %slice.168), channel_id=1, source_target_pairs={{0,8},{8,16},{16,24},{24,0},{32,40},{40,48},{48,56},{56,32},{64,72... | collective-permute-start | bytes 393224 | tf_op jit(solution)/shard_map/ppermute | solution.py:138
  23.2 5.0 %collective-permute-start.4 = (bf16[1,256,256]{2,1,0:T(8,128)(2,1)S(1)}, bf16[1,256,256]{2,1,0:T(8,128)(2,1)S(1)}, u32[]{:S(2)}, u32[]{:S(2)}) collective-permute-start(bf16[1,256,256]{2,1,0:T(8,128)(2,1)S(1)} %slice.169), channel_id=1, source_target_pairs={{0,24},{8,0},{16,8},{24,16},{32,56},{40,32},{48,40},{56,48},{64,88... | collective-permute-start | bytes 393224 | tf_op jit(solution)/shard_map/ppermute | solution.py:139
  28.3 29.8 %copy-start.8 = (s32[1,1,2,256]{3,2,1,0:T(2,128)S(1)}, s32[1,1,2,256]{3,2,1,0:T(2,128)}, u32[]{:S(2)}) copy-start(s32[1,1,2,256]{3,2,1,0:T(2,128)} %param.9) | copy-start | bytes 6148
  29.6 23.6 %collective-permute-start.6 = (bf16[8,256,256]{2,1,0:T(8,128)(2,1)S(1)}, bf16[8,256,256]{2,1,0:T(8,128)(2,1)S(1)}, u32[]{:S(2)}, u32[]{:S(2)}) collective-permute-start(bf16[8,256,256]{2,1,0:T(8,128)(2,1)S(1)} %bitcast.177), channel_id=1, source_target_pairs={{0,64},{8,72},{16,80},{24,88},{32,96},{40,104},{48,112},{56,120},{... | collective-permute-start | bytes 3145736 | tf_op jit(solution)/shard_map/ppermute | solution.py:136
  31.1 23.1 %collective-permute-start.5 = (bf16[8,256,256]{2,1,0:T(8,128)(2,1)S(1)}, bf16[8,256,256]{2,1,0:T(8,128)(2,1)S(1)}, u32[]{:S(2)}, u32[]{:S(2)}) collective-permute-start(bf16[8,256,256]{2,1,0:T(8,128)(2,1)S(1)} %bitcast.178), channel_id=1, source_target_pairs={{0,192},{8,200},{16,208},{24,216},{32,224},{40,232},{48,240},{56,2... | collective-permute-start | bytes 3145736 | tf_op jit(solution)/shard_map/ppermute | solution.py:137
  54.0 11.7 %collective-permute-start.7 = (bf16[4,256,256]{2,1,0:T(8,128)(2,1)}, bf16[4,256,256]{2,1,0:T(8,128)(2,1)}, u32[]{:S(2)}, u32[]{:S(2)}) collective-permute-start(bf16[4,256,256]{2,1,0:T(8,128)(2,1)} %slice.170), channel_id=1, source_target_pairs={{0,64},{8,72},{16,80},{24,88},{32,96},{40,104},{48,112},{56,120},{... | collective-permute-start | bytes 1572872 | tf_op jit(solution)/shard_map/ppermute | solution.py:138
  55.1 10.7 %collective-permute-start.8 = (bf16[4,256,256]{2,1,0:T(8,128)(2,1)}, bf16[4,256,256]{2,1,0:T(8,128)(2,1)}, u32[]{:S(2)}, u32[]{:S(2)}) collective-permute-start(bf16[4,256,256]{2,1,0:T(8,128)(2,1)} %slice.171), channel_id=1, source_target_pairs={{0,192},{8,200},{16,208},{24,216},{32,224},{40,232},{48,240},{56,2... | collective-permute-start | bytes 1572872 | tf_op jit(solution)/shard_map/ppermute | solution.py:139
  82.9 2.9 collective-permute-start.9
  87.2 34.8 %copy-start.9 = (bf16[1,1,256,256]{3,2,1,0:T(8,128)(2,1)S(1)}, bf16[1,1,256,256]{3,2,1,0:T(8,128)(2,1)}, u32[]{:S(2)}) copy-start(bf16[1,1,256,256]{3,2,1,0:T(8,128)(2,1)} %param.13) | copy-start | bytes 393220
  87.3 15.0 %collective-permute-start.10 = (f32[256,256]{1,0:T(8,128)S(1)}, f32[256,256]{1,0:T(8,128)S(1)}, u32[]{:S(2)}, u32[]{:S(2)}) collective-permute-start(f32[256,256]{1,0:T(8,128)S(1)} %get-tuple-element.19), channel_id=1, source_target_pairs={{0,2},{1,3},{2,4},{3,5},{4,6},{5,7},{6,0},{7,1},{8,10},{9,11},{10,... | collective-permute-start | bytes 786440 | tf_op jit(solution)/shard_map/ppermute | solution.py:159
  90.4 26.8 %collective-permute-start.11 = (f32[256,256]{1,0:T(8,128)S(1)}, f32[256,256]{1,0:T(8,128)S(1)}, u32[]{:S(2)}, u32[]{:S(2)}) collective-permute-start(f32[256,256]{1,0:T(8,128)S(1)} %get-tuple-element.21), channel_id=1, source_target_pairs={{0,4},{1,5},{2,6},{3,7},{4,0},{5,1},{6,2},{7,3},{8,12},{9,13},{10,... | collective-permute-start | bytes 786440 | tf_op jit(solution)/shard_map/ppermute | solution.py:159
  99.2 22.8 %collective-permute-start.12 = (f32[256,256]{1,0:T(8,128)S(1)}, f32[256,256]{1,0:T(8,128)S(1)}, u32[]{:S(2)}, u32[]{:S(2)}) collective-permute-start(f32[256,256]{1,0:T(8,128)S(1)} %get-tuple-element.20), channel_id=1, source_target_pairs={{0,6},{1,7},{2,0},{3,1},{4,2},{5,3},{6,4},{7,5},{8,14},{9,15},{10,... | collective-permute-start | bytes 786440 | tf_op jit(solution)/shard_map/ppermute | solution.py:159
  123.2 1.4 collective-permute-start.13
  124.7 20.5 %collective-permute-start.14 = (bf16[2,256,256]{2,1,0:T(8,128)(2,1)S(1)}, bf16[2,256,256]{2,1,0:T(8,128)(2,1)S(1)}, u32[]{:S(2)}, u32[]{:S(2)}) collective-permute-start(bf16[2,256,256]{2,1,0:T(8,128)(2,1)S(1)} %get-tuple-element.24), channel_id=1, source_target_pairs={{0,6},{1,7},{2,0},{3,1},{4,2},{5,3},{6,4},{7,5},{8,14},{9,15},{10,... | collective-permute-start | bytes 786440 | tf_op jit(solution)/shard_map/ppermute | solution.py:149
  127.3 22.7 %collective-permute-start.15 = (bf16[2,256,256]{2,1,0:T(8,128)(2,1)S(1)}, bf16[2,256,256]{2,1,0:T(8,128)(2,1)S(1)}, u32[]{:S(2)}, u32[]{:S(2)}) collective-permute-start(bf16[2,256,256]{2,1,0:T(8,128)(2,1)S(1)} %get-tuple-element.24), channel_id=1, source_target_pairs={{0,4},{1,5},{2,6},{3,7},{4,0},{5,1},{6,2},{7,3},{8,12},{9,13},{10,... | collective-permute-start | bytes 786440 | tf_op jit(solution)/shard_map/ppermute | solution.py:149
  127.3 22.7 %collective-permute-start.16 = (bf16[2,256,256]{2,1,0:T(8,128)(2,1)S(1)}, bf16[2,256,256]{2,1,0:T(8,128)(2,1)S(1)}, u32[]{:S(2)}, u32[]{:S(2)}) collective-permute-start(bf16[2,256,256]{2,1,0:T(8,128)(2,1)S(1)} %get-tuple-element.24), channel_id=1, source_target_pairs={{0,2},{1,3},{2,4},{3,5},{4,6},{5,7},{6,0},{7,1},{8,10},{9,11},{10,... | collective-permute-start | bytes 786440 | tf_op jit(solution)/shard_map/ppermute | solution.py:149
  164.6 1.4 copy-start.2
  166.0 47.9 %collective-permute-start.25 = (bf16[6,2,256,128]{3,2,1,0:T(8,128)(2,1)S(1)}, bf16[6,2,256,128]{3,2,1,0:T(8,128)(2,1)S(1)}, u32[]{:S(2)}, u32[]{:S(2)}) collective-permute-start(bf16[6,2,256,128]{3,2,1,0:T(8,128)(2,1)S(1)} %pad_maximum_fusion.2), channel_id=1, source_target_pairs={{0,8},{8,16},{16,24},{24,0},{32,40},{40,48},{48,56},{56,32},{64,72... | collective-permute-start | bytes 2359304 | tf_op jit(solution)/shard_map/ppermute | solution.py:102
  191.2 23.5 %collective-permute-start.26 = (bf16[6,2,256,128]{3,2,1,0:T(8,128)(2,1)S(1)}, bf16[6,2,256,128]{3,2,1,0:T(8,128)(2,1)S(1)}, u32[]{:S(2)}, u32[]{:S(2)}) collective-permute-start(bf16[6,2,256,128]{3,2,1,0:T(8,128)(2,1)S(1)} %pad_maximum_fusion.3), channel_id=1, source_target_pairs={{0,24},{8,0},{16,8},{24,16},{32,56},{40,32},{48,40},{56,48},{64,88... | collective-permute-start | bytes 2359304 | tf_op jit(solution)/shard_map/ppermute | solution.py:103
  204.4 70.7 %collective-permute-start.17 = (bf16[12,256,128]{2,1,0:T(8,128)(2,1)S(1)}, bf16[12,256,128]{2,1,0:T(8,128)(2,1)}, u32[]{:S(2)}, u32[]{:S(2)}) collective-permute-start(bf16[12,256,128]{2,1,0:T(8,128)(2,1)S(1)} %pad_maximum_fusion), channel_id=1, source_target_pairs={{0,64},{8,72},{16,80},{24,88},{32,96},{40,104},{48,112},{56,120},{... | collective-permute-start | bytes 2359304 | tf_op jit(solution)/shard_map/ppermute | solution.py:102
  205.4 72.2 %collective-permute-start.18 = (bf16[12,256,128]{2,1,0:T(8,128)(2,1)}, bf16[12,256,128]{2,1,0:T(8,128)(2,1)}, u32[]{:S(2)}, u32[]{:S(2)}) collective-permute-start(bf16[12,256,128]{2,1,0:T(8,128)(2,1)} %pad_maximum_fusion.1), channel_id=1, source_target_pairs={{0,192},{8,200},{16,208},{24,216},{32,224},{40,232},{48,240},{56,2... | collective-permute-start | bytes 2359304 | tf_op jit(solution)/shard_map/ppermute | solution.py:103
  213.9 1.0 copy-start.4
  214.7 65.7 %collective-permute-start.27 = (bf16[2,2,256,128]{3,2,1,0:T(8,128)(2,1)}, bf16[2,2,256,128]{3,2,1,0:T(8,128)(2,1)}, u32[]{:S(2)}, u32[]{:S(2)}) collective-permute-start(bf16[2,2,256,128]{3,2,1,0:T(8,128)(2,1)} %slice.188), channel_id=1, source_target_pairs={{0,8},{8,16},{16,24},{24,0},{32,40},{40,48},{48,56},{56,32},{64,72... | collective-permute-start | bytes 786440 | tf_op jit(solution)/shard_map/ppermute | solution.py:104
  215.0 1.0 copy-start.5
  216.0 64.5 %collective-permute-start.28 = (bf16[2,2,256,128]{3,2,1,0:T(8,128)(2,1)}, bf16[2,2,256,128]{3,2,1,0:T(8,128)(2,1)}, u32[]{:S(2)}, u32[]{:S(2)}) collective-permute-start(bf16[2,2,256,128]{3,2,1,0:T(8,128)(2,1)} %slice.189), channel_id=1, source_target_pairs={{0,24},{8,0},{16,8},{24,16},{32,56},{40,32},{48,40},{56,48},{64,88... | collective-permute-start | bytes 786440 | tf_op jit(solution)/shard_map/ppermute | solution.py:105
  229.2 68.7 %all-to-all-start = ((f32[256,1,256]{2,1,0:T(1,128)}), f32[256,1,256]{2,1,0:T(1,128)S(1)}, u32[]{:S(2)}, u32[]{:S(2)}) async-start(f32[256,1,256]{2,1,0:T(1,128)} %copy.21), calls=%async_computation | async-start | bytes 524288 | tf_op jit(solution)/shard_map/all_to_all | solution.py:206
  276.1 11.9 %collective-permute-start.19 = (bf16[4,256,128]{2,1,0:T(8,128)(2,1)S(1)}, bf16[4,256,128]{2,1,0:T(8,128)(2,1)S(1)}, u32[]{:S(2)}, u32[]{:S(2)}) collective-permute-start(bf16[4,256,128]{2,1,0:T(8,128)(2,1)S(1)} %slice.175), channel_id=1, source_target_pairs={{0,64},{8,72},{16,80},{24,88},{32,96},{40,104},{48,112},{56,120},{... | collective-permute-start | bytes 786440 | tf_op jit(solution)/shard_map/ppermute | solution.py:104
  278.6 9.9 %collective-permute-start.20 = (bf16[4,256,128]{2,1,0:T(8,128)(2,1)S(1)}, bf16[4,256,128]{2,1,0:T(8,128)(2,1)S(1)}, u32[]{:S(2)}, u32[]{:S(2)}) collective-permute-start(bf16[4,256,128]{2,1,0:T(8,128)(2,1)S(1)} %slice.176), channel_id=1, source_target_pairs={{0,192},{8,200},{16,208},{24,216},{32,224},{40,232},{48,240},{56,2... | collective-permute-start | bytes 786440 | tf_op jit(solution)/shard_map/ppermute | solution.py:105
  282.3 11.0 %collective-permute-start.29 = (bf16[3,256,128]{2,1,0:T(8,128)(2,1)S(1)}, bf16[3,256,128]{2,1,0:T(8,128)(2,1)S(1)}, u32[]{:S(2)}, u32[]{:S(2)}) collective-permute-start(bf16[3,256,128]{2,1,0:T(8,128)(2,1)S(1)} %pad_maximum_fusion.8), channel_id=1, source_target_pairs={{0,64},{8,72},{16,80},{24,88},{32,96},{40,104},{48,112},{56,120},{... | collective-permute-start | bytes 589832 | tf_op jit(solution)/shard_map/ppermute | solution.py:102
  282.7 12.8 %collective-permute-start.30 = (bf16[3,256,128]{2,1,0:T(8,128)(2,1)S(1)}, bf16[3,256,128]{2,1,0:T(8,128)(2,1)S(1)}, u32[]{:S(2)}, u32[]{:S(2)}) collective-permute-start(bf16[3,256,128]{2,1,0:T(8,128)(2,1)S(1)} %pad_maximum_fusion.9), channel_id=1, source_target_pairs={{0,192},{8,200},{16,208},{24,216},{32,224},{40,232},{48,240},{56,2... | collective-permute-start | bytes 589832 | tf_op jit(solution)/shard_map/ppermute | solution.py:103
  290.0 1.0 copy-start.3
  291.1 19.7 %collective-permute-start.21 = (bf16[3,256,128]{2,1,0:T(8,128)(2,1)S(1)}, bf16[3,256,128]{2,1,0:T(8,128)(2,1)S(1)}, u32[]{:S(2)}, u32[]{:S(2)}) collective-permute-start(bf16[3,256,128]{2,1,0:T(8,128)(2,1)S(1)} %pad_maximum_fusion.6), channel_id=1, source_target_pairs={{0,8},{8,16},{16,24},{24,0},{32,40},{40,48},{48,56},{56,32},{64,72... | collective-permute-start | bytes 589832 | tf_op jit(solution)/shard_map/ppermute | solution.py:102
  292.8 19.7 %collective-permute-start.22 = (bf16[3,256,128]{2,1,0:T(8,128)(2,1)S(1)}, bf16[3,256,128]{2,1,0:T(8,128)(2,1)S(1)}, u32[]{:S(2)}, u32[]{:S(2)}) collective-permute-start(bf16[3,256,128]{2,1,0:T(8,128)(2,1)S(1)} %pad_maximum_fusion.7), channel_id=1, source_target_pairs={{0,24},{8,0},{16,8},{24,16},{32,56},{40,32},{48,40},{56,48},{64,88... | collective-permute-start | bytes 589832 | tf_op jit(solution)/shard_map/ppermute | solution.py:103
  293.3 0.7 copy-start.6
  294.0 19.0 %collective-permute-start.31 = (bf16[1,256,128]{2,1,0:T(8,128)(2,1)S(1)}, bf16[1,256,128]{2,1,0:T(8,128)(2,1)S(1)}, u32[]{:S(2)}, u32[]{:S(2)}) collective-permute-start(bf16[1,256,128]{2,1,0:T(8,128)(2,1)S(1)} %slice.194), channel_id=1, source_target_pairs={{0,64},{8,72},{16,80},{24,88},{32,96},{40,104},{48,112},{56,120},{... | collective-permute-start | bytes 196616 | tf_op jit(solution)/shard_map/ppermute | solution.py:104
  295.6 0.7 copy-start.7
  296.2 16.8 %collective-permute-start.32 = (bf16[1,256,128]{2,1,0:T(8,128)(2,1)S(1)}, bf16[1,256,128]{2,1,0:T(8,128)(2,1)S(1)}, u32[]{:S(2)}, u32[]{:S(2)}) collective-permute-start(bf16[1,256,128]{2,1,0:T(8,128)(2,1)S(1)} %slice.195), channel_id=1, source_target_pairs={{0,192},{8,200},{16,208},{24,216},{32,224},{40,232},{48,240},{56,2... | collective-permute-start | bytes 196616 | tf_op jit(solution)/shard_map/ppermute | solution.py:105
  299.1 25.0 %all-to-all-start.1 = ((f32[256,1,256]{2,1,0:T(1,128)}), f32[256,1,256]{2,1,0:T(1,128)S(1)}, u32[]{:S(2)}, u32[]{:S(2)}) async-start(f32[256,1,256]{2,1,0:T(1,128)} %broadcast_in_dim.2), calls=%async_computation.1 | async-start | bytes 524288 | tf_op jit(solution)/shard_map/all_to_all | solution.py:208
  310.8 19.5 %copy-start.1 = (bf16[256,256]{1,0:T(8,128)(2,1)S(1)}, bf16[256,256]{1,0:T(8,128)(2,1)}, u32[]{:S(2)}) copy-start(bf16[256,256]{1,0:T(8,128)(2,1)} %param.12) | copy-start | bytes 393220
  310.8 5.0 %collective-permute-start.23 = (bf16[1,256,128]{2,1,0:T(8,128)(2,1)S(1)}, bf16[1,256,128]{2,1,0:T(8,128)(2,1)S(1)}, u32[]{:S(2)}, u32[]{:S(2)}) collective-permute-start(bf16[1,256,128]{2,1,0:T(8,128)(2,1)S(1)} %slice.181), channel_id=1, source_target_pairs={{0,8},{8,16},{16,24},{24,0},{32,40},{40,48},{48,56},{56,32},{64,72... | collective-permute-start | bytes 196616 | tf_op jit(solution)/shard_map/ppermute | solution.py:104
  312.4 4.7 %collective-permute-start.24 = (bf16[1,256,128]{2,1,0:T(8,128)(2,1)S(1)}, bf16[1,256,128]{2,1,0:T(8,128)(2,1)S(1)}, u32[]{:S(2)}, u32[]{:S(2)}) collective-permute-start(bf16[1,256,128]{2,1,0:T(8,128)(2,1)S(1)} %slice.182), channel_id=1, source_target_pairs={{0,24},{8,0},{16,8},{24,16},{32,56},{40,32},{48,40},{56,48},{64,88... | collective-permute-start | bytes 196616 | tf_op jit(solution)/shard_map/ppermute | solution.py:105
  318.2 11.4 %collective-permute-start.33 = (bf16[256,256]{1,0:T(8,128)(2,1)S(1)}, bf16[256,256]{1,0:T(8,128)(2,1)S(1)}, u32[]{:S(2)}, u32[]{:S(2)}) collective-permute-start(bf16[256,256]{1,0:T(8,128)(2,1)S(1)} %fusion.40), channel_id=1, source_target_pairs={{0,32},{8,40},{16,48},{24,56},{32,0},{40,8},{48,16},{56,24},{64,96... | collective-permute-start | bytes 393224 | tf_op jit(solution)/shard_map/ppermute | solution.py:117

commit v5 on v4

--- a/solution.py
+++ b/solution.py
@@ -5,55 +5,37 @@
 from jax.experimental.pallas import tpu as pltpu
 from jax.sharding import PartitionSpec as P
 
-GROUP = 32
-
 
 def tile_aggregate(values, pick_index, place_index, live_count, source, segments, transposed, out_dtype):
     slot_total, tile_side, _ = values.shape
     width = source.shape[2]
-    steps = slot_total // GROUP
 
     def kernel(picks_ref, places_ref, count_ref, vals_ref, src_ref, out_ref, acc_ref):
-        step = pl.program_id(0)
-
-        @pl.when(step == 0)
-        def _():
-            acc_ref[...] = jnp.zeros_like(acc_ref)
-
-        def slot(j, carry):
-            k = step * GROUP + j
-
-            @pl.when(k < count_ref[0])
-            def _():
-                src_tile = src_ref[picks_ref[k]]
-                tile = vals_ref[j]
-                if transposed:
-                    term = lax.dot_general(tile, src_tile, (((0,), (0,)), ((), ())),
-                                           preferred_element_type=jnp.float32)
-                else:
-                    term = jnp.dot(tile, src_tile, preferred_element_type=jnp.float32)
-                place = places_ref[k]
-                acc_ref[place] += term
-
+        acc_ref[...] = jnp.zeros_like(acc_ref)
+
+        def slot(k, carry):
+            src_tile = src_ref[picks_ref[k]]
+            tile = vals_ref[k]
+            if transposed:
+                term = lax.dot_general(tile, src_tile, (((0,), (0,)), ((), ())),
+                                       preferred_element_type=jnp.float32)
+            else:
+                term = jnp.dot(tile, src_tile, preferred_element_type=jnp.float32)
+            acc_ref[places_ref[k]] += term
             return carry
 
-        lax.fori_loop(0, GROUP, slot, 0)
-
-        @pl.when(step == steps - 1)
-        def _():
-            out_ref[...] = acc_ref[...].astype(out_ref.dtype)
-
-    def vals_map(i, picks, places, count):
-        return (jnp.minimum(i, (count[0] - 1) // GROUP), 0, 0)
-
+        lax.fori_loop(0, count_ref[0], slot, 0)
+        out_ref[...] = acc_ref[...].astype(out_ref.dtype)
+
+    whole = lambda i, *_: (0, 0, 0)
     grid_spec = pltpu.PrefetchScalarGridSpec(
         num_scalar_prefetch=3,
-        grid=(steps,),
+        grid=(1,),
         in_specs=[
-            pl.BlockSpec((GROUP, tile_side, tile_side), vals_map),
-            pl.BlockSpec(source.shape, lambda i, *_: (0, 0, 0)),
+            pl.BlockSpec(values.shape, whole, pipeline_mode=pl.Buffered(1)),
+            pl.BlockSpec(source.shape, whole, pipeline_mode=pl.Buffered(1)),
         ],
-        out_specs=pl.BlockSpec((segments, tile_side, width), lambda i, *_: (0, 0, 0)),
+        out_specs=pl.BlockSpec((segments, tile_side, width), whole, pipeline_mode=pl.Buffered(1)),
         scratch_shapes=[pltpu.VMEM((segments, tile_side, width), jnp.float32)],
     )
     flops = 2 * slot_total * tile_side * tile_side * width
@@ -61,9 +43,7 @@
         kernel,
         grid_spec=grid_spec,
         out_shape=jax.ShapeDtypeStruct((segments, tile_side, width), out_dtype),
-        compiler_params=pltpu.CompilerParams(
-            dimension_semantics=("arbitrary",), vmem_limit_bytes=48 * 1024 * 1024
-        ),
+        compiler_params=pltpu.CompilerParams(vmem_limit_bytes=56 * 1024 * 1024),
         cost_estimate=pl.CostEstimate(
             flops=flops, transcendentals=0,
             bytes_accessed=values.size * 2 + source.size * 2 + segments * tile_side * width * jnp.dtype(out_dtype).itemsize,

time: 337 us -> 335 us (level); the launches traced: 330 us -> 333 us
  starting transfers between devices: 166 us -> 161 us
  local copies, waits for them, and re-layouts: 15.9 us -> 19.4 us
    ppermute x4, starting transfers between devices: 19.8 us -> 51 us  [ring_reduce(): from_right = lax.ppermute(to_left, axis_name, leftward)]
    all_to_all x1, starting transfers between devices: 45.9 us -> 15.8 us  [all_sum(): lax.all_to_all(pieces, axes, 0, 0, tiled=True)]
    ppermute x4, starting transfers between devices: 27.2 us -> 9.5 us  [ring_reduce(): from_left = lax.ppermute(to_right, axis_name, rightward)]
    ppermute x3, starting transfers between devices: 14.9 us -> 25.5 us  [line_reduce(): lax.ppermute(outgoing.astype(link_dtype), axis_name, ring_step_pairs(size...]
    ppermute x4, starting transfers between devices: 16.1 us -> 5.86 us  [ring_reduce(): relay_right = lax.ppermute(from_right[lead:], axis_name, leftward)]
    ppermute x1, starting transfers between devices: 0.09 us -> 10.1 us  [col_reduce(): lax.ppermute(other, 'col', [(index, index ^ 1) for index in range(size)])]
where the time goes in v5:
time: 335 us; the launch traced here: 333 us
  starting transfers between devices  161 us (48%)
  waiting for transfers between devices  108 us (32%)
  Pallas kernels  25.4 us (8%)
  local copies, waits for them, and re-layouts  19.4 us (6%)
  other arithmetic  16 us (5%)
    ppermute x4, starting transfers between devices, ring_reduce(): from_right = lax.ppermute(to_left, axis_name, leftward)  51 us
    ppermute x2, waiting for transfers between devices, ring_gather(): from_left = lax.ppermute(block, axis_name, rightward)  25.7 us
    ppermute x3, starting transfers between devices, line_reduce(): lax.ppermute(outgoing.astype(link_dtype), axis_name, ring_step_pairs(size...  25.5 us
    pallas_call x2, Pallas kernels, tile_aggregate(): pl.pallas_call(kernel, grid_spec=grid_spec, out_shape=jax.ShapeDtypeStruc...  25.4 us
    ppermute x3, waiting for transfers between devices, line_gather(): lax.ppermute(block, axis_name, ring_step_pairs(size, stride, 4, shift))  21.2 us
    ppermute x3, waiting for transfers between devices, line_reduce(): lax.ppermute(outgoing.astype(link_dtype), axis_name, ring_step_pairs(size...  19.9 us
    all_to_all x1, starting transfers between devices, all_sum(): lax.all_to_all(pieces, axes, 0, 0, tiled=True)  15.8 us
    all_to_all x1, starting transfers between devices, all_sum(): return lax.all_to_all(spread, axes, 0, 0, tiled=True).reshape(rows, width)  11.7 us
  transfers between devices with their start and end apart: 36, of which 20 were waited for; matrix products, arithmetic and copies ran while one was open for 5% of the time, Pallas kernels for 0%

profile of v5, /device:TPU:72, one launch (start us, length us, event | category | flops | bytes accessed | tf_op | source)
XLA Modules:
  0.0 333.4 jit_solution(9558140955392397481)
XLA Ops:
  0.6 5.5 %collective-permute-start = (bf16[256,256]{1,0:T(8,128)(2,1)}, bf16[256,256]{1,0:T(8,128)(2,1)S(1)}, u32[]{:S(2)}, u32[]{:S(2)}) collective-permute-start(bf16[256,256]{1,0:T(8,128)(2,1)} %bitcast.190), channel_id=1, source_target_pairs={{0,32},{8,40},{16,48},{24,56},{32,0},{40,8},{48,16},{56,24},{64,96... | collective-permute-start | bytes 393224 | tf_op jit(solution)/shard_map/ppermute | solution.py:106
  6.1 6.9 %collective-permute-done = bf16[256,256]{1,0:T(8,128)(2,1)S(1)} collective-permute-done((bf16[256,256]{1,0:T(8,128)(2,1)}, bf16[256,256]{1,0:T(8,128)(2,1)S(1)}, u32[]{:S(2)}, u32[]{:S(2)}) %collective-permute-start) | collective-permute-done | bytes 131104 | tf_op jit(solution)/shard_map/ppermute | solution.py:106
  14.0 1.7 collective-permute-start.2
  16.1 5.4 %collective-permute-done.2 = bf16[2,256,256]{2,1,0:T(8,128)(2,1)S(1)} collective-permute-done((bf16[2,256,256]{2,1,0:T(8,128)(2,1)S(1)}, bf16[2,256,256]{2,1,0:T(8,128)(2,1)S(1)}, u32[]{:S(2)}, u32[]{:S(2)}) %collective-permute-start.2) | collective-permute-done | bytes 262176 | tf_op jit(solution)/shard_map/ppermute | solution.py:116
  21.6 1.7 collective-permute-start.3
  23.8 2.8 collective-permute-done.3
  26.6 1.7 collective-permute-done.4
  28.3 1.3 fusion.10
  29.6 1.6 collective-permute-start.6
  31.1 1.7 collective-permute-start.5
  32.9 20.3 %collective-permute-done.6 = bf16[8,256,256]{2,1,0:T(8,128)(2,1)S(1)} collective-permute-done((bf16[8,256,256]{2,1,0:T(8,128)(2,1)S(1)}, bf16[8,256,256]{2,1,0:T(8,128)(2,1)S(1)}, u32[]{:S(2)}, u32[]{:S(2)}) %collective-permute-start.6) | collective-permute-done | bytes 1048608 | tf_op jit(solution)/shard_map/ppermute | solution.py:116
  55.1 3.0 collective-permute-start.8
  59.5 6.3 %collective-permute-done.7 = bf16[4,256,256]{2,1,0:T(8,128)(2,1)} collective-permute-done((bf16[4,256,256]{2,1,0:T(8,128)(2,1)}, bf16[4,256,256]{2,1,0:T(8,128)(2,1)}, u32[]{:S(2)}, u32[]{:S(2)}) %collective-permute-start.7) | collective-permute-done | bytes 524320 | tf_op jit(solution)/shard_map/ppermute | solution.py:118
  65.9 1.3 fusion.18
  67.4 1.3 fusion.19
  68.7 2.3 constant_dynamic-slice_fusion
  71.0 11.8 %shard_map.85 = f32[16,128,256]{2,1,0:T(8,128)} custom-call(s32[256]{0:T(256)} %bitcast.193, s32[256]{0:T(256)} %bitcast.191, s32[1]{0:T(128)} %bitcast.164.count_ref, bf16[256,128,128]{2,1,0:T(8,128)(2,1)} %bitcast.166, bf16[64,128,256]{2,1,0:T(8,128)(2,1)} %bitcast.169), custom_call_target="tpu_custom_call" | custom-call | flops 2147483648 | bytes 14680064 | tf_op jit(solution)/shard_map/pallas_call | solution.py:42
  82.8 1.4 dynamic-slice_bitcast_fusion
  84.2 10.1 %collective-permute-start.9 = (f32[4,256,256]{2,1,0:T(8,128)S(1)}, f32[4,256,256]{2,1,0:T(8,128)}, u32[]{:S(2)}, u32[]{:S(2)}) collective-permute-start(f32[4,256,256]{2,1,0:T(8,128)S(1)} %dynamic-slice_bitcast_fusion), channel_id=1, source_target_pairs={{0,1},{1,0},{2,3},{3,2},{4,5},{5,4},{6,7},{7,6},{8,9},{9,8},{10,11... | collective-permute-start | bytes 3145736 | tf_op jit(solution)/shard_map/ppermute | solution.py:162
  94.3 2.4 collective-permute-done.9
  96.7 1.4 bitcast_add_fusion
  98.3 22.6 %collective-permute-start.11 = (f32[256,256]{1,0:T(8,128)S(1)}, f32[256,256]{1,0:T(8,128)S(1)}, u32[]{:S(2)}, u32[]{:S(2)}) collective-permute-start(f32[256,256]{1,0:T(8,128)S(1)} %get-tuple-element.21), channel_id=1, source_target_pairs={{0,4},{1,5},{2,6},{3,7},{4,0},{5,1},{6,2},{7,3},{8,12},{9,13},{10,... | collective-permute-start | bytes 786440 | tf_op jit(solution)/shard_map/ppermute | solution.py:139
  120.8 2.8 collective-permute-start.12
  123.7 15.1 %collective-permute-done.11 = f32[256,256]{1,0:T(8,128)S(1)} collective-permute-done((f32[256,256]{1,0:T(8,128)S(1)}, f32[256,256]{1,0:T(8,128)S(1)}, u32[]{:S(2)}, u32[]{:S(2)}) %collective-permute-start.11) | collective-permute-done | bytes 262176 | tf_op jit(solution)/shard_map/ppermute | solution.py:139
  138.8 4.8 %collective-permute-done.12 = f32[256,256]{1,0:T(8,128)S(1)} collective-permute-done((f32[256,256]{1,0:T(8,128)S(1)}, f32[256,256]{1,0:T(8,128)S(1)}, u32[]{:S(2)}, u32[]{:S(2)}) %collective-permute-start.12) | collective-permute-done | bytes 262176 | tf_op jit(solution)/shard_map/ppermute | solution.py:139
  143.7 0.9 fusion.27
  144.9 1.3 collective-permute-done.13
  146.3 2.6 collective-permute-start.14
  148.9 1.6 collective-permute-start.16
  150.5 16.4 %collective-permute-done.14 = bf16[2,256,256]{2,1,0:T(8,128)(2,1)S(1)} collective-permute-done((bf16[2,256,256]{2,1,0:T(8,128)(2,1)S(1)}, bf16[2,256,256]{2,1,0:T(8,128)(2,1)S(1)}, u32[]{:S(2)}, u32[]{:S(2)}) %collective-permute-start.14) | collective-permute-done | bytes 262176 | tf_op jit(solution)/shard_map/ppermute | solution.py:129
  166.8 4.8 %collective-permute-done.15 = bf16[2,256,256]{2,1,0:T(8,128)(2,1)S(1)} collective-permute-done((bf16[2,256,256]{2,1,0:T(8,128)(2,1)S(1)}, bf16[2,256,256]{2,1,0:T(8,128)(2,1)S(1)}, u32[]{:S(2)}, u32[]{:S(2)}) %collective-permute-start.15) | collective-permute-done | bytes 262176 | tf_op jit(solution)/shard_map/ppermute | solution.py:129
  171.6 2.2 fusion.3
  173.9 13.7 %shard_map.86 = bf16[64,128,256]{2,1,0:T(8,128)(2,1)} custom-call(s32[256]{0:T(256)} %bitcast.192, s32[256]{0:T(256)} %bitcast.194, s32[1]{0:T(128)} %bitcast.165.count_ref, bf16[256,128,128]{2,1,0:T(8,128)(2,1)} %bitcast.167, bf16[16,128,256]{2,1,0:T(8,128)(2,1)} %bitcast.181), custom_call_target="tpu_custom_call" | custom-call | flops 2147483648 | bytes 13631488 | tf_op jit(solution)/shard_map/pallas_call | solution.py:42
  187.5 2.6 fusion.44
  190.3 1.2 copy-done.3
  191.6 7.4 %collective-permute-start.25 = (bf16[6,2,256,128]{3,2,1,0:T(8,128)(2,1)S(1)}, bf16[6,2,256,128]{3,2,1,0:T(8,128)(2,1)S(1)}, u32[]{:S(2)}, u32[]{:S(2)}) collective-permute-start(bf16[6,2,256,128]{3,2,1,0:T(8,128)(2,1)S(1)} %pad_maximum_fusion.2), channel_id=1, source_target_pairs={{0,8},{8,16},{16,24},{24,0},{32,40},{40,48},{48,56},{56,32},{64,72... | collective-permute-start | bytes 2359304 | tf_op jit(solution)/shard_map/ppermute | solution.py:82
  199.1 44.2 %collective-permute-start.26 = (bf16[6,2,256,128]{3,2,1,0:T(8,128)(2,1)S(1)}, bf16[6,2,256,128]{3,2,1,0:T(8,128)(2,1)S(1)}, u32[]{:S(2)}, u32[]{:S(2)}) collective-permute-start(bf16[6,2,256,128]{3,2,1,0:T(8,128)(2,1)S(1)} %pad_maximum_fusion.3), channel_id=1, source_target_pairs={{0,24},{8,0},{16,8},{24,16},{32,56},{40,32},{48,40},{56,48},{64,88... | collective-permute-start | bytes 2359304 | tf_op jit(solution)/shard_map/ppermute | solution.py:83
  243.6 1.0 pad_maximum_fusion.1
  244.5 3.2 collective-permute-start.18
  247.8 8.1 %collective-permute-done.25 = bf16[6,2,256,128]{3,2,1,0:T(8,128)(2,1)S(1)} collective-permute-done((bf16[6,2,256,128]{3,2,1,0:T(8,128)(2,1)S(1)}, bf16[6,2,256,128]{3,2,1,0:T(8,128)(2,1)S(1)}, u32[]{:S(2)}, u32[]{:S(2)}) %collective-permute-start.25) | collective-permute-done | bytes 786464 | tf_op jit(solution)/shard_map/ppermute | solution.py:82
  256.6 1.7 collective-permute-start.27
  259.3 1.8 collective-permute-start.28
  261.3 1.0 copy.21
  262.3 15.8 %all-to-all-start = ((f32[256,1,256]{2,1,0:T(1,128)}), f32[256,1,256]{2,1,0:T(1,128)S(1)}, u32[]{:S(2)}, u32[]{:S(2)}) async-start(f32[256,1,256]{2,1,0:T(1,128)} %copy.21), calls=%async_computation | async-start | bytes 524288 | tf_op jit(solution)/shard_map/all_to_all | solution.py:186
  278.2 1.0 slice.175
  279.2 1.6 collective-permute-start.19
  280.7 1.0 slice.176
  281.7 1.8 collective-permute-start.20
  283.5 1.8 fusion.15
  285.8 3.0 collective-permute-start.30
  288.8 2.2 collective-permute-done.19
  291.6 1.4 fusion.17
  293.0 1.0 copy-done.4
  294.2 1.6 collective-permute-start.21
  297.1 1.5 collective-permute-start.31
  299.3 1.7 collective-permute-start.32
  302.1 11.7 %all-to-all-start.1 = ((f32[256,1,256]{2,1,0:T(1,128)}), f32[256,1,256]{2,1,0:T(1,128)S(1)}, u32[]{:S(2)}, u32[]{:S(2)}) async-start(f32[256,1,256]{2,1,0:T(1,128)} %broadcast_in_dim.2), calls=%async_computation.1 | async-start | bytes 524288 | tf_op jit(solution)/shard_map/all_to_all | solution.py:188
  313.9 1.6 collective-permute-start.23
  316.1 1.0 fusion.29
  317.1 1.8 collective-permute-done.23
  318.9 1.3 collective-permute-done.24
  320.2 1.0 fusion.31
  321.3 5.1 %collective-permute-start.33 = (bf16[256,256]{1,0:T(8,128)(2,1)S(1)}, bf16[256,256]{1,0:T(8,128)(2,1)S(1)}, u32[]{:S(2)}, u32[]{:S(2)}) collective-permute-start(bf16[256,256]{1,0:T(8,128)(2,1)S(1)} %fusion.40), channel_id=1, source_target_pairs={{0,32},{8,40},{16,48},{24,56},{32,0},{40,8},{48,16},{56,24},{64,96... | collective-permute-start | bytes 393224 | tf_op jit(solution)/shard_map/ppermute | solution.py:97
  327.8 4.8 %collective-permute-done.33 = bf16[256,256]{1,0:T(8,128)(2,1)S(1)} collective-permute-done((bf16[256,256]{1,0:T(8,128)(2,1)S(1)}, bf16[256,256]{1,0:T(8,128)(2,1)S(1)}, u32[]{:S(2)}, u32[]{:S(2)}) %collective-permute-start.33) | collective-permute-done | bytes 131104 | tf_op jit(solution)/shard_map/ppermute | solution.py:97
  (95 shorter events, 15.3 us)
Async XLA Ops:
  0.6 143.0 %copy-start = (bf16[256,256]{1,0:T(8,128)(2,1)S(1)}, bf16[256,256]{1,0:T(8,128)(2,1)}, u32[]{:S(2)}) copy-start(bf16[256,256]{1,0:T(8,128)(2,1)} %param.12) | copy-start | bytes 393220
  0.6 12.4 %collective-permute-start = (bf16[256,256]{1,0:T(8,128)(2,1)}, bf16[256,256]{1,0:T(8,128)(2,1)S(1)}, u32[]{:S(2)}, u32[]{:S(2)}) collective-permute-start(bf16[256,256]{1,0:T(8,128)(2,1)} %bitcast.190), channel_id=1, source_target_pairs={{0,32},{8,40},{16,48},{24,56},{32,0},{40,8},{48,16},{56,24},{64,96... | collective-permute-start | bytes 393224 | tf_op jit(solution)/shard_map/ppermute | solution.py:106
  14.0 7.5 %collective-permute-start.2 = (bf16[2,256,256]{2,1,0:T(8,128)(2,1)S(1)}, bf16[2,256,256]{2,1,0:T(8,128)(2,1)S(1)}, u32[]{:S(2)}, u32[]{:S(2)}) collective-permute-start(bf16[2,256,256]{2,1,0:T(8,128)(2,1)S(1)} %get-tuple-element.30), channel_id=1, source_target_pairs={{0,8},{8,16},{16,24},{24,0},{32,40},{40,48},{48,56},{56,32},{64,72... | collective-permute-start | bytes 786440 | tf_op jit(solution)/shard_map/ppermute | solution.py:116
  15.7 7.5 %collective-permute-start.1 = (bf16[2,256,256]{2,1,0:T(8,128)(2,1)S(1)}, bf16[2,256,256]{2,1,0:T(8,128)(2,1)S(1)}, u32[]{:S(2)}, u32[]{:S(2)}) collective-permute-start(bf16[2,256,256]{2,1,0:T(8,128)(2,1)S(1)} %get-tuple-element.30), channel_id=1, source_target_pairs={{0,24},{8,0},{16,8},{24,16},{32,56},{40,32},{48,40},{56,48},{64,88... | collective-permute-start | bytes 786440 | tf_op jit(solution)/shard_map/ppermute | solution.py:117
  21.6 5.0 %collective-permute-start.3 = (bf16[1,256,256]{2,1,0:T(8,128)(2,1)S(1)}, bf16[1,256,256]{2,1,0:T(8,128)(2,1)S(1)}, u32[]{:S(2)}, u32[]{:S(2)}) collective-permute-start(bf16[1,256,256]{2,1,0:T(8,128)(2,1)S(1)} %slice.168), channel_id=1, source_target_pairs={{0,8},{8,16},{16,24},{24,0},{32,40},{40,48},{48,56},{56,32},{64,72... | collective-permute-start | bytes 393224 | tf_op jit(solution)/shard_map/ppermute | solution.py:118
  23.2 5.0 %collective-permute-start.4 = (bf16[1,256,256]{2,1,0:T(8,128)(2,1)S(1)}, bf16[1,256,256]{2,1,0:T(8,128)(2,1)S(1)}, u32[]{:S(2)}, u32[]{:S(2)}) collective-permute-start(bf16[1,256,256]{2,1,0:T(8,128)(2,1)S(1)} %slice.169), channel_id=1, source_target_pairs={{0,24},{8,0},{16,8},{24,16},{32,56},{40,32},{48,40},{56,48},{64,88... | collective-permute-start | bytes 393224 | tf_op jit(solution)/shard_map/ppermute | solution.py:119
  28.3 29.8 %copy-start.9 = (s32[1,1,2,256]{3,2,1,0:T(2,128)S(1)}, s32[1,1,2,256]{3,2,1,0:T(2,128)}, u32[]{:S(2)}) copy-start(s32[1,1,2,256]{3,2,1,0:T(2,128)} %param.9) | copy-start | bytes 6148
  29.6 23.6 %collective-permute-start.6 = (bf16[8,256,256]{2,1,0:T(8,128)(2,1)S(1)}, bf16[8,256,256]{2,1,0:T(8,128)(2,1)S(1)}, u32[]{:S(2)}, u32[]{:S(2)}) collective-permute-start(bf16[8,256,256]{2,1,0:T(8,128)(2,1)S(1)} %bitcast.170), channel_id=1, source_target_pairs={{0,64},{8,72},{16,80},{24,88},{32,96},{40,104},{48,112},{56,120},{... | collective-permute-start | bytes 3145736 | tf_op jit(solution)/shard_map/ppermute | solution.py:116
  31.1 23.1 %collective-permute-start.5 = (bf16[8,256,256]{2,1,0:T(8,128)(2,1)S(1)}, bf16[8,256,256]{2,1,0:T(8,128)(2,1)S(1)}, u32[]{:S(2)}, u32[]{:S(2)}) collective-permute-start(bf16[8,256,256]{2,1,0:T(8,128)(2,1)S(1)} %bitcast.171), channel_id=1, source_target_pairs={{0,192},{8,200},{16,208},{24,216},{32,224},{40,232},{48,240},{56,2... | collective-permute-start | bytes 3145736 | tf_op jit(solution)/shard_map/ppermute | solution.py:117
  54.0 11.7 %collective-permute-start.7 = (bf16[4,256,256]{2,1,0:T(8,128)(2,1)}, bf16[4,256,256]{2,1,0:T(8,128)(2,1)}, u32[]{:S(2)}, u32[]{:S(2)}) collective-permute-start(bf16[4,256,256]{2,1,0:T(8,128)(2,1)} %slice.170), channel_id=1, source_target_pairs={{0,64},{8,72},{16,80},{24,88},{32,96},{40,104},{48,112},{56,120},{... | collective-permute-start | bytes 1572872 | tf_op jit(solution)/shard_map/ppermute | solution.py:118
  55.1 10.7 %collective-permute-start.8 = (bf16[4,256,256]{2,1,0:T(8,128)(2,1)}, bf16[4,256,256]{2,1,0:T(8,128)(2,1)}, u32[]{:S(2)}, u32[]{:S(2)}) collective-permute-start(bf16[4,256,256]{2,1,0:T(8,128)(2,1)} %slice.171), channel_id=1, source_target_pairs={{0,192},{8,200},{16,208},{24,216},{32,224},{40,232},{48,240},{56,2... | collective-permute-start | bytes 1572872 | tf_op jit(solution)/shard_map/ppermute | solution.py:119
  82.8 13.9 %copy-start.2 = (f32[16,128,256]{2,1,0:T(8,128)S(1)}, f32[16,128,256]{2,1,0:T(8,128)}, u32[]{:S(2)}) copy-start(f32[16,128,256]{2,1,0:T(8,128)} %shard_map.85) | copy-start | bytes 6291460
  84.2 12.5 %collective-permute-start.9 = (f32[4,256,256]{2,1,0:T(8,128)S(1)}, f32[4,256,256]{2,1,0:T(8,128)}, u32[]{:S(2)}, u32[]{:S(2)}) collective-permute-start(f32[4,256,256]{2,1,0:T(8,128)S(1)} %dynamic-slice_bitcast_fusion), channel_id=1, source_target_pairs={{0,1},{1,0},{2,3},{3,2},{4,5},{5,4},{6,7},{7,6},{8,9},{9,8},{10,11... | collective-permute-start | bytes 3145736 | tf_op jit(solution)/shard_map/ppermute | solution.py:162
  98.1 45.6 %copy-start.10 = (bf16[1,1,256,256]{3,2,1,0:T(8,128)(2,1)S(1)}, bf16[1,1,256,256]{3,2,1,0:T(8,128)(2,1)}, u32[]{:S(2)}) copy-start(bf16[1,1,256,256]{3,2,1,0:T(8,128)(2,1)} %param.13) | copy-start | bytes 393220
  98.2 25.5 %collective-permute-start.10 = (f32[256,256]{1,0:T(8,128)S(1)}, f32[256,256]{1,0:T(8,128)S(1)}, u32[]{:S(2)}, u32[]{:S(2)}) collective-permute-start(f32[256,256]{1,0:T(8,128)S(1)} %get-tuple-element.19), channel_id=1, source_target_pairs={{0,2},{1,3},{2,4},{3,5},{4,6},{5,7},{6,0},{7,1},{8,10},{9,11},{10,... | collective-permute-start | bytes 786440 | tf_op jit(solution)/shard_map/ppermute | solution.py:139
  98.3 40.5 %collective-permute-start.11 = (f32[256,256]{1,0:T(8,128)S(1)}, f32[256,256]{1,0:T(8,128)S(1)}, u32[]{:S(2)}, u32[]{:S(2)}) collective-permute-start(f32[256,256]{1,0:T(8,128)S(1)} %get-tuple-element.21), channel_id=1, source_target_pairs={{0,4},{1,5},{2,6},{3,7},{4,0},{5,1},{6,2},{7,3},{8,12},{9,13},{10,... | collective-permute-start | bytes 786440 | tf_op jit(solution)/shard_map/ppermute | solution.py:139
  120.8 22.8 %collective-permute-start.12 = (f32[256,256]{1,0:T(8,128)S(1)}, f32[256,256]{1,0:T(8,128)S(1)}, u32[]{:S(2)}, u32[]{:S(2)}) collective-permute-start(f32[256,256]{1,0:T(8,128)S(1)} %get-tuple-element.20), channel_id=1, source_target_pairs={{0,6},{1,7},{2,0},{3,1},{4,2},{5,3},{6,4},{7,5},{8,14},{9,15},{10,... | collective-permute-start | bytes 786440 | tf_op jit(solution)/shard_map/ppermute | solution.py:139
  144.8 1.4 collective-permute-start.13
  146.3 20.5 %collective-permute-start.14 = (bf16[2,256,256]{2,1,0:T(8,128)(2,1)S(1)}, bf16[2,256,256]{2,1,0:T(8,128)(2,1)S(1)}, u32[]{:S(2)}, u32[]{:S(2)}) collective-permute-start(bf16[2,256,256]{2,1,0:T(8,128)(2,1)S(1)} %get-tuple-element.24), channel_id=1, source_target_pairs={{0,6},{1,7},{2,0},{3,1},{4,2},{5,3},{6,4},{7,5},{8,14},{9,15},{10,... | collective-permute-start | bytes 786440 | tf_op jit(solution)/shard_map/ppermute | solution.py:129
  148.9 22.7 %collective-permute-start.15 = (bf16[2,256,256]{2,1,0:T(8,128)(2,1)S(1)}, bf16[2,256,256]{2,1,0:T(8,128)(2,1)S(1)}, u32[]{:S(2)}, u32[]{:S(2)}) collective-permute-start(bf16[2,256,256]{2,1,0:T(8,128)(2,1)S(1)} %get-tuple-element.24), channel_id=1, source_target_pairs={{0,4},{1,5},{2,6},{3,7},{4,0},{5,1},{6,2},{7,3},{8,12},{9,13},{10,... | collective-permute-start | bytes 786440 | tf_op jit(solution)/shard_map/ppermute | solution.py:129
  148.9 22.7 %collective-permute-start.16 = (bf16[2,256,256]{2,1,0:T(8,128)(2,1)S(1)}, bf16[2,256,256]{2,1,0:T(8,128)(2,1)S(1)}, u32[]{:S(2)}, u32[]{:S(2)}) collective-permute-start(bf16[2,256,256]{2,1,0:T(8,128)(2,1)S(1)} %get-tuple-element.24), channel_id=1, source_target_pairs={{0,2},{1,3},{2,4},{3,5},{4,6},{5,7},{6,0},{7,1},{8,10},{9,11},{10,... | collective-permute-start | bytes 786440 | tf_op jit(solution)/shard_map/ppermute | solution.py:129
  190.1 1.4 copy-start.3
  191.6 64.3 %collective-permute-start.25 = (bf16[6,2,256,128]{3,2,1,0:T(8,128)(2,1)S(1)}, bf16[6,2,256,128]{3,2,1,0:T(8,128)(2,1)S(1)}, u32[]{:S(2)}, u32[]{:S(2)}) collective-permute-start(bf16[6,2,256,128]{3,2,1,0:T(8,128)(2,1)S(1)} %pad_maximum_fusion.2), channel_id=1, source_target_pairs={{0,8},{8,16},{16,24},{24,0},{32,40},{40,48},{48,56},{56,32},{64,72... | collective-permute-start | bytes 2359304 | tf_op jit(solution)/shard_map/ppermute | solution.py:82
  199.1 59.2 %collective-permute-start.26 = (bf16[6,2,256,128]{3,2,1,0:T(8,128)(2,1)S(1)}, bf16[6,2,256,128]{3,2,1,0:T(8,128)(2,1)S(1)}, u32[]{:S(2)}, u32[]{:S(2)}) collective-permute-start(bf16[6,2,256,128]{3,2,1,0:T(8,128)(2,1)S(1)} %pad_maximum_fusion.3), channel_id=1, source_target_pairs={{0,24},{8,0},{16,8},{24,16},{32,56},{40,32},{48,40},{56,48},{64,88... | collective-permute-start | bytes 2359304 | tf_op jit(solution)/shard_map/ppermute | solution.py:83
  243.5 34.7 %collective-permute-start.17 = (bf16[12,256,128]{2,1,0:T(8,128)(2,1)S(1)}, bf16[12,256,128]{2,1,0:T(8,128)(2,1)}, u32[]{:S(2)}, u32[]{:S(2)}) collective-permute-start(bf16[12,256,128]{2,1,0:T(8,128)(2,1)S(1)} %pad_maximum_fusion), channel_id=1, source_target_pairs={{0,64},{8,72},{16,80},{24,88},{32,96},{40,104},{48,112},{56,120},{... | collective-permute-start | bytes 2359304 | tf_op jit(solution)/shard_map/ppermute | solution.py:82
  244.5 36.2 %collective-permute-start.18 = (bf16[12,256,128]{2,1,0:T(8,128)(2,1)}, bf16[12,256,128]{2,1,0:T(8,128)(2,1)}, u32[]{:S(2)}, u32[]{:S(2)}) collective-permute-start(bf16[12,256,128]{2,1,0:T(8,128)(2,1)} %pad_maximum_fusion.1), channel_id=1, source_target_pairs={{0,192},{8,200},{16,208},{24,216},{32,224},{40,232},{48,240},{56,2... | collective-permute-start | bytes 2359304 | tf_op jit(solution)/shard_map/ppermute | solution.py:83
  255.9 2.5 copy-start.5
  256.6 26.9 %collective-permute-start.27 = (bf16[2,2,256,128]{3,2,1,0:T(8,128)(2,1)}, bf16[2,2,256,128]{3,2,1,0:T(8,128)(2,1)}, u32[]{:S(2)}, u32[]{:S(2)}) collective-permute-start(bf16[2,2,256,128]{3,2,1,0:T(8,128)(2,1)} %slice.188), channel_id=1, source_target_pairs={{0,8},{8,16},{16,24},{24,0},{32,40},{40,48},{48,56},{56,32},{64,72... | collective-permute-start | bytes 786440 | tf_op jit(solution)/shard_map/ppermute | solution.py:84
  258.3 1.0 copy-start.6
  259.3 24.2 %collective-permute-start.28 = (bf16[2,2,256,128]{3,2,1,0:T(8,128)(2,1)}, bf16[2,2,256,128]{3,2,1,0:T(8,128)(2,1)}, u32[]{:S(2)}, u32[]{:S(2)}) collective-permute-start(bf16[2,2,256,128]{3,2,1,0:T(8,128)(2,1)} %slice.189), channel_id=1, source_target_pairs={{0,24},{8,0},{16,8},{24,16},{32,56},{40,32},{48,40},{56,48},{64,88... | collective-permute-start | bytes 786440 | tf_op jit(solution)/shard_map/ppermute | solution.py:85
  262.3 38.7 %all-to-all-start = ((f32[256,1,256]{2,1,0:T(1,128)}), f32[256,1,256]{2,1,0:T(1,128)S(1)}, u32[]{:S(2)}, u32[]{:S(2)}) async-start(f32[256,1,256]{2,1,0:T(1,128)} %copy.21), calls=%async_computation | async-start | bytes 524288 | tf_op jit(solution)/shard_map/all_to_all | solution.py:186
  279.2 11.9 %collective-permute-start.19 = (bf16[4,256,128]{2,1,0:T(8,128)(2,1)S(1)}, bf16[4,256,128]{2,1,0:T(8,128)(2,1)S(1)}, u32[]{:S(2)}, u32[]{:S(2)}) collective-permute-start(bf16[4,256,128]{2,1,0:T(8,128)(2,1)S(1)} %slice.175), channel_id=1, source_target_pairs={{0,64},{8,72},{16,80},{24,88},{32,96},{40,104},{48,112},{56,120},{... | collective-permute-start | bytes 786440 | tf_op jit(solution)/shard_map/ppermute | solution.py:84
  281.7 9.9 %collective-permute-start.20 = (bf16[4,256,128]{2,1,0:T(8,128)(2,1)S(1)}, bf16[4,256,128]{2,1,0:T(8,128)(2,1)S(1)}, u32[]{:S(2)}, u32[]{:S(2)}) collective-permute-start(bf16[4,256,128]{2,1,0:T(8,128)(2,1)S(1)} %slice.176), channel_id=1, source_target_pairs={{0,192},{8,200},{16,208},{24,216},{32,224},{40,232},{48,240},{56,2... | collective-permute-start | bytes 786440 | tf_op jit(solution)/shard_map/ppermute | solution.py:85
  285.4 11.0 %collective-permute-start.29 = (bf16[3,256,128]{2,1,0:T(8,128)(2,1)S(1)}, bf16[3,256,128]{2,1,0:T(8,128)(2,1)S(1)}, u32[]{:S(2)}, u32[]{:S(2)}) collective-permute-start(bf16[3,256,128]{2,1,0:T(8,128)(2,1)S(1)} %pad_maximum_fusion.8), channel_id=1, source_target_pairs={{0,64},{8,72},{16,80},{24,88},{32,96},{40,104},{48,112},{56,120},{... | collective-permute-start | bytes 589832 | tf_op jit(solution)/shard_map/ppermute | solution.py:82
  285.8 12.8 %collective-permute-start.30 = (bf16[3,256,128]{2,1,0:T(8,128)(2,1)S(1)}, bf16[3,256,128]{2,1,0:T(8,128)(2,1)S(1)}, u32[]{:S(2)}, u32[]{:S(2)}) collective-permute-start(bf16[3,256,128]{2,1,0:T(8,128)(2,1)S(1)} %pad_maximum_fusion.9), channel_id=1, source_target_pairs={{0,192},{8,200},{16,208},{24,216},{32,224},{40,232},{48,240},{56,2... | collective-permute-start | bytes 589832 | tf_op jit(solution)/shard_map/ppermute | solution.py:83
  293.0 1.0 copy-start.4
  294.2 19.7 %collective-permute-start.21 = (bf16[3,256,128]{2,1,0:T(8,128)(2,1)S(1)}, bf16[3,256,128]{2,1,0:T(8,128)(2,1)S(1)}, u32[]{:S(2)}, u32[]{:S(2)}) collective-permute-start(bf16[3,256,128]{2,1,0:T(8,128)(2,1)S(1)} %pad_maximum_fusion.6), channel_id=1, source_target_pairs={{0,8},{8,16},{16,24},{24,0},{32,40},{40,48},{48,56},{56,32},{64,72... | collective-permute-start | bytes 589832 | tf_op jit(solution)/shard_map/ppermute | solution.py:82
  295.8 19.7 %collective-permute-start.22 = (bf16[3,256,128]{2,1,0:T(8,128)(2,1)S(1)}, bf16[3,256,128]{2,1,0:T(8,128)(2,1)S(1)}, u32[]{:S(2)}, u32[]{:S(2)}) collective-permute-start(bf16[3,256,128]{2,1,0:T(8,128)(2,1)S(1)} %pad_maximum_fusion.7), channel_id=1, source_target_pairs={{0,24},{8,0},{16,8},{24,16},{32,56},{40,32},{48,40},{56,48},{64,88... | collective-permute-start | bytes 589832 | tf_op jit(solution)/shard_map/ppermute | solution.py:83
  296.4 0.7 copy-start.7
  297.1 19.0 %collective-permute-start.31 = (bf16[1,256,128]{2,1,0:T(8,128)(2,1)S(1)}, bf16[1,256,128]{2,1,0:T(8,128)(2,1)S(1)}, u32[]{:S(2)}, u32[]{:S(2)}) collective-permute-start(bf16[1,256,128]{2,1,0:T(8,128)(2,1)S(1)} %slice.194), channel_id=1, source_target_pairs={{0,64},{8,72},{16,80},{24,88},{32,96},{40,104},{48,112},{56,120},{... | collective-permute-start | bytes 196616 | tf_op jit(solution)/shard_map/ppermute | solution.py:84
  298.6 0.7 copy-start.8
  299.3 16.8 %collective-permute-start.32 = (bf16[1,256,128]{2,1,0:T(8,128)(2,1)S(1)}, bf16[1,256,128]{2,1,0:T(8,128)(2,1)S(1)}, u32[]{:S(2)}, u32[]{:S(2)}) collective-permute-start(bf16[1,256,128]{2,1,0:T(8,128)(2,1)S(1)} %slice.195), channel_id=1, source_target_pairs={{0,192},{8,200},{16,208},{24,216},{32,224},{40,232},{48,240},{56,2... | collective-permute-start | bytes 196616 | tf_op jit(solution)/shard_map/ppermute | solution.py:85
  302.1 24.9 %all-to-all-start.1 = ((f32[256,1,256]{2,1,0:T(1,128)}), f32[256,1,256]{2,1,0:T(1,128)S(1)}, u32[]{:S(2)}, u32[]{:S(2)}) async-start(f32[256,1,256]{2,1,0:T(1,128)} %broadcast_in_dim.2), calls=%async_computation.1 | async-start | bytes 524288 | tf_op jit(solution)/shard_map/all_to_all | solution.py:188
  313.8 19.5 %copy-start.1 = (bf16[256,256]{1,0:T(8,128)(2,1)S(1)}, bf16[256,256]{1,0:T(8,128)(2,1)}, u32[]{:S(2)}) copy-start(bf16[256,256]{1,0:T(8,128)(2,1)} %param.12) | copy-start | bytes 393220
  313.9 5.0 %collective-permute-start.23 = (bf16[1,256,128]{2,1,0:T(8,128)(2,1)S(1)}, bf16[1,256,128]{2,1,0:T(8,128)(2,1)S(1)}, u32[]{:S(2)}, u32[]{:S(2)}) collective-permute-start(bf16[1,256,128]{2,1,0:T(8,128)(2,1)S(1)} %slice.181), channel_id=1, source_target_pairs={{0,8},{8,16},{16,24},{24,0},{32,40},{40,48},{48,56},{56,32},{64,72... | collective-permute-start | bytes 196616 | tf_op jit(solution)/shard_map/ppermute | solution.py:84
  315.5 4.7 %collective-permute-start.24 = (bf16[1,256,128]{2,1,0:T(8,128)(2,1)S(1)}, bf16[1,256,128]{2,1,0:T(8,128)(2,1)S(1)}, u32[]{:S(2)}, u32[]{:S(2)}) collective-permute-start(bf16[1,256,128]{2,1,0:T(8,128)(2,1)S(1)} %slice.182), channel_id=1, source_target_pairs={{0,24},{8,0},{16,8},{24,16},{32,56},{40,32},{48,40},{56,48},{64,88... | collective-permute-start | bytes 196616 | tf_op jit(solution)/shard_map/ppermute | solution.py:85
  321.3 11.4 %collective-permute-start.33 = (bf16[256,256]{1,0:T(8,128)(2,1)S(1)}, bf16[256,256]{1,0:T(8,128)(2,1)S(1)}, u32[]{:S(2)}, u32[]{:S(2)}) collective-permute-start(bf16[256,256]{1,0:T(8,128)(2,1)S(1)} %fusion.40), channel_id=1, source_target_pairs={{0,32},{8,40},{16,48},{24,56},{32,0},{40,8},{48,16},{56,24},{64,96... | collective-permute-start | bytes 393224 | tf_op jit(solution)/shard_map/ppermute | solution.py:97
